TPU v7x, 32 devices: a whole 2x2x4 slice. The times are simulated.
32 devices in a mesh: dom: 8 (over z, core), loop: 4 (over y, x).
Axes of the slice: x: 2, y: 2, z: 4, core: 2. Of those that a mesh axis runs over, the one named last changes fastest.
Arguments:
- cotangent: bfloat16 [32768, 256], P(('dom', 'loop')), may hold values from -6 to 6
- preact: bfloat16 [32768, 256], P(('dom', 'loop')), may hold values from -6 to 6
- aggregated: bfloat16 [32768, 256], P(('dom', 'loop')), may hold values from -6 to 6
- weight: bfloat16 [256, 256], replicated, may hold values from -0.375 to 0.375
- tile_values: bfloat16 [20480, 128, 128], P(('dom', 'loop')), as said below
- tile_rows: int32 [32, 640], P(('dom', 'loop')), may hold values from 0 to 31
- tile_cols: int32 [32, 640], P(('dom', 'loop')), may hold values from 0 to 63, as said below
- tile_counts: int32 [32], P(('dom', 'loop')), may hold values from 32 to 640
Outputs:
- node_grad: float32 [32768, 256], P(('dom', 'loop'))
- weight_grad: float32 [256, 256], replicated
Inputs may be any that keep to these rules, and one draw needn't show every extreme that they name: `tile_cols`: the live tiles of one device touch, for every dom index, exactly 4 distinct column blocks, and every tile's column lies among them. `tile_values`: entries are nonnegative.
All inputs are finite; a program needn't handle non-finite values.
Results may differ from a plain program's by a relative error of at most 0.0029.
Values may be sent and summed in bfloat16 or wider, within the bound.
No kernel may reach another device: no remote copies, remote signals or barrier semaphores. Data moves between devices by JAX's collectives and lax.ppermute only.
A program may use at most 192 MiB of HBM per device.

v0:
```python
import math

import jax
import jax.numpy as jnp
from jax import lax
from jax.experimental import pallas as pl
from jax.experimental.pallas import tpu as pltpu
from jax.sharding import PartitionSpec as P

GROUP = 32
CAP = 4


def _spmm_kernel(rows_ref, slots_ref, cnt_ref, tv_ref, part_ref, out_ref):
    g = pl.program_id(0)
    count = cnt_ref[0]
    group = tv_ref.shape[0]
    base = g * group

    @pl.when(g == 0)
    def _():
        out_ref[...] = jnp.zeros(out_ref.shape, out_ref.dtype)

    @pl.when(base < count)
    def _():
        for t in range(group):
            j = base + t
            r = rows_ref[j]
            c = slots_ref[j]
            term = lax.dot_general(
                tv_ref[t],
                part_ref[r],
                (((0,), (0,)), ((), ())),
                preferred_element_type=jnp.float32,
            )
            out_ref[c] += jnp.where(j < count, term, 0.0)


def _spmm(rows, slots, count, tile_values, partition, out_blocks):
    tiles, tile_size, _ = tile_values.shape
    part_blocks, _, width = partition.shape
    group = math.gcd(tiles, GROUP)

    def tv_map(g, rows_ref, slots_ref, cnt_ref):
        last = jnp.maximum((cnt_ref[0] + group - 1) // group - 1, 0)
        return (jnp.minimum(g, last), 0, 0)

    def whole(g, rows_ref, slots_ref, cnt_ref):
        return (0, 0, 0)

    return pl.pallas_call(
        _spmm_kernel,
        out_shape=jax.ShapeDtypeStruct((out_blocks, tile_size, width), jnp.float32),
        grid_spec=pltpu.PrefetchScalarGridSpec(
            num_scalar_prefetch=3,
            grid=(tiles // group,),
            in_specs=[
                pl.BlockSpec((group, tile_size, tile_size), tv_map),
                pl.BlockSpec((part_blocks, tile_size, width), whole),
            ],
            out_specs=pl.BlockSpec((out_blocks, tile_size, width), whole),
        ),
        compiler_params=pltpu.CompilerParams(
            dimension_semantics=("arbitrary",),
            vmem_limit_bytes=50 * 1024 * 1024,
        ),
    )(rows, slots, count, tile_values, partition)


def _combine_kernel(map_ref, recv_ref, out_ref):
    g = pl.program_id(0)
    per = recv_ref.shape[0]

    @pl.when(g == 0)
    def _():
        out_ref[...] = jnp.zeros(out_ref.shape, out_ref.dtype)

    for k in range(per):
        b = map_ref[g * per + k]
        out_ref[b] += recv_ref[k]


def _combine(block_map, received, out_blocks):
    total, tile_size, width = received.shape
    per = CAP

    def recv_map(g, map_ref):
        return (g, 0, 0)

    def whole(g, map_ref):
        return (0, 0, 0)

    return pl.pallas_call(
        _combine_kernel,
        out_shape=jax.ShapeDtypeStruct((out_blocks, tile_size, width), jnp.float32),
        grid_spec=pltpu.PrefetchScalarGridSpec(
            num_scalar_prefetch=1,
            grid=(total // per,),
            in_specs=[pl.BlockSpec((per, tile_size, width), recv_map)],
            out_specs=pl.BlockSpec((out_blocks, tile_size, width), whole),
        ),
        compiler_params=pltpu.CompilerParams(dimension_semantics=("arbitrary",)),
    )(block_map, received)


def _pick(stacked, index):
    return lax.dynamic_index_in_dim(stacked, index, axis=0, keepdims=False)


def shards(cotangent, preact, aggregated, weight, tile_values, tile_rows, tile_cols, tile_counts):
    node_rows, width = cotangent.shape
    tile_size = tile_values.shape[1]
    dom_count = lax.axis_size("dom")
    loop_count = lax.axis_size("loop")
    dom_index = lax.axis_index("dom")
    loop_index = lax.axis_index("loop")
    total_nodes = node_rows * dom_count * loop_count
    local_blocks = node_rows // tile_size
    tile_total = tile_rows.shape[1]

    masked = jnp.where(preact > 0, cotangent, jnp.zeros_like(cotangent))
    weight_term = jnp.dot(aggregated.T, masked, preferred_element_type=jnp.float32) * (
        1.0 / math.sqrt(total_nodes)
    )
    projected = jnp.dot(masked, weight.T, preferred_element_type=jnp.float32).astype(jnp.bfloat16)

    pieces = [projected]
    terms = [weight_term]
    for shift in range(1, loop_count):
        pairs = [(i, (i + shift) % loop_count) for i in range(loop_count)]
        piece, term = lax.ppermute((projected, weight_term), "loop", pairs)
        pieces.append(piece)
        terms.append(term)
    partition = jnp.concatenate(pieces, axis=0).reshape(
        loop_count * local_blocks, tile_size, width
    )
    terms = jnp.stack(terms)
    loop_sum = _pick(terms, loop_index % loop_count)
    for source in range(1, loop_count):
        loop_sum = loop_sum + _pick(terms, (loop_index - source) % loop_count)

    rows = tile_rows[0]
    source_loop = rows // local_blocks
    rows = ((loop_index - source_loop) % loop_count) * local_blocks + rows % local_blocks

    cols = tile_cols[0]
    live = jnp.arange(tile_total, dtype=jnp.int32) < tile_counts[0]
    all_blocks = dom_count * local_blocks
    onehot = cols[:, None] == jnp.arange(all_blocks, dtype=jnp.int32)[None, :]
    present = jnp.any(onehot & live[:, None], axis=0).reshape(dom_count, local_blocks)
    present = present.astype(jnp.int32)
    rank = jnp.cumsum(present, axis=1) - 1
    tile_rank = jnp.sum(jnp.where(onehot, rank.reshape(1, -1), 0), axis=1)
    tile_rank = jnp.clip(tile_rank, 0, CAP - 1)
    block_ids = jnp.arange(local_blocks, dtype=jnp.int32)
    table = jnp.stack(
        [jnp.sum(jnp.where((rank == k) & (present > 0), block_ids[None, :], 0), axis=1) for k in range(CAP)],
        axis=1,
    )
    dom_ids = jnp.arange(dom_count, dtype=jnp.int32)
    rotate = ((dom_ids[:, None] + dom_index) % dom_count) == dom_ids[None, :]
    table = jnp.sum(jnp.where(rotate[:, :, None], table[None, :, :], 0), axis=1)
    dest_dom = cols // local_blocks
    slots = ((dest_dom - dom_index) % dom_count) * CAP + tile_rank

    compact = _spmm(rows, slots, tile_counts, tile_values, partition, dom_count * CAP)

    chunk = width // dom_count
    chunks = loop_sum.reshape(dom_count, chunk, width)
    received = [compact[:CAP]]
    maps = [table[0]]
    parts = [_pick(chunks, dom_index)]
    for shift in range(1, dom_count):
        pairs = [(i, (i + shift) % dom_count) for i in range(dom_count)]
        slab, ids, part = lax.ppermute(
            (compact[shift * CAP:(shift + 1) * CAP], table[shift], _pick(chunks, (dom_index + shift) % dom_count)),
            "dom",
            pairs,
        )
        received.append(slab)
        maps.append(ids)
        parts.append(part)
    parts = jnp.stack(parts)
    own = _pick(parts, dom_index % dom_count)
    for source in range(1, dom_count):
        own = own + _pick(parts, (dom_index - source) % dom_count)
    gathered = [own]
    for shift in range(1, dom_count):
        pairs = [(i, (i + shift) % dom_count) for i in range(dom_count)]
        gathered.append(lax.ppermute(own, "dom", pairs))
    gathered = jnp.stack(gathered)
    weight_grad = jnp.concatenate(
        [_pick(gathered, (dom_index - k) % dom_count) for k in range(dom_count)], axis=0
    )
    node_grad = _combine(
        jnp.concatenate(maps), jnp.concatenate(received, axis=0), local_blocks
    ).reshape(node_rows, width)
    return (node_grad, weight_grad)


def solution(mesh):
    return jax.shard_map(
        shards,
        mesh=mesh,
        in_specs=(
            P(("dom", "loop"), None),
            P(("dom", "loop"), None),
            P(("dom", "loop"), None),
            P(),
            P(("dom", "loop"), None, None),
            P(("dom", "loop"), None),
            P(("dom", "loop"), None),
            P(("dom", "loop")),
        ),
        out_specs=(P(("dom", "loop"), None), P()),
        check_vma=False,
    )
```

profile of v0, /device:TPU:9, one launch (start us, length us, event | category | flops | bytes accessed | tf_op | source)
XLA Modules:
  0.0 238.7 jit_solution(4594009329830194987)
XLA Ops:
  2.3 2.2 collective-permute-start.9
  11.7 9.1 %collective-permute-done.19 = f32[256,256]{1,0:T(8,128)S(1)} collective-permute-done((f32[256,256]{1,0:T(8,128)S(1)}, f32[256,256]{1,0:T(8,128)S(1)}, u32[]{:S(2)}, u32[]{:S(2)}) %collective-permute-start.19) | collective-permute-done | bytes 262176 | tf_op jit(solution)/shard_map/ppermute | solution.py:131
  23.5 19.0 %collective-permute-start = (s32[4]{0:T(128)S(1)}, s32[4]{0:T(128)S(1)}, u32[]{:S(2)}, u32[]{:S(2)}) collective-permute-start(s32[4]{0:T(128)S(1)} %get-tuple-element.12), channel_id=1, source_target_pairs={{0,4},{4,8},{8,12},{12,16},{16,20},{20,24},{24,28},{28,0},{1,5},{5... | collective-permute-start | bytes 56 | tf_op jit(solution)/shard_map/ppermute | solution.py:175
  47.7 4.3 %collective-permute-start.22 = (f32[32,256]{1,0:T(8,128)S(1)}, f32[32,256]{1,0:T(8,128)S(1)}, u32[]{:S(2)}, u32[]{:S(2)}) collective-permute-start(f32[32,256]{1,0:T(8,128)S(1)} %get-tuple-element.28), channel_id=1, source_target_pairs={{0,12},{4,16},{8,20},{12,24},{16,28},{20,0},{24,4},{28,8},{1,13},{... | collective-permute-start | bytes 98312 | tf_op jit(solution)/shard_map/ppermute | solution.py:175
  52.0 3.1 %collective-permute-done.22 = f32[32,256]{1,0:T(8,128)S(1)} collective-permute-done((f32[32,256]{1,0:T(8,128)S(1)}, f32[32,256]{1,0:T(8,128)S(1)}, u32[]{:S(2)}, u32[]{:S(2)}) %collective-permute-start.22) | collective-permute-done | bytes 32800 | tf_op jit(solution)/shard_map/ppermute | solution.py:175
  55.0 4.3 %collective-permute-done.23 = f32[32,256]{1,0:T(8,128)S(1)} collective-permute-done((f32[32,256]{1,0:T(8,128)S(1)}, f32[32,256]{1,0:T(8,128)S(1)}, u32[]{:S(2)}, u32[]{:S(2)}) %collective-permute-start.23) | collective-permute-done | bytes 32800 | tf_op jit(solution)/shard_map/ppermute | solution.py:175
  59.3 3.2 %collective-permute-start.24 = (f32[32,256]{1,0:T(8,128)S(1)}, f32[32,256]{1,0:T(8,128)S(1)}, u32[]{:S(2)}, u32[]{:S(2)}) collective-permute-start(f32[32,256]{1,0:T(8,128)S(1)} %get-tuple-element.26), channel_id=1, source_target_pairs={{0,20},{4,24},{8,28},{12,0},{16,4},{20,8},{24,12},{28,16},{1,21},{... | collective-permute-start | bytes 98312 | tf_op jit(solution)/shard_map/ppermute | solution.py:175
  63.9 2.8 %collective-permute-done.25 = f32[32,256]{1,0:T(8,128)S(1)} collective-permute-done((f32[32,256]{1,0:T(8,128)S(1)}, f32[32,256]{1,0:T(8,128)S(1)}, u32[]{:S(2)}, u32[]{:S(2)}) %collective-permute-start.25) | collective-permute-done | bytes 32800 | tf_op jit(solution)/shard_map/ppermute | solution.py:175
  67.8 2.7 %collective-permute-done.26 = f32[32,256]{1,0:T(8,128)S(1)} collective-permute-done((f32[32,256]{1,0:T(8,128)S(1)}, f32[32,256]{1,0:T(8,128)S(1)}, u32[]{:S(2)}, u32[]{:S(2)}) %collective-permute-start.26) | collective-permute-done | bytes 32800 | tf_op jit(solution)/shard_map/ppermute | solution.py:175
  70.7 3.5 %collective-permute-start.1 = (s32[4]{0:T(128)S(1)}, s32[4]{0:T(128)S(1)}, u32[]{:S(2)}, u32[]{:S(2)}) collective-permute-start(s32[4]{0:T(128)S(1)} %get-tuple-element.11), channel_id=1, source_target_pairs={{0,8},{4,12},{8,16},{12,20},{16,24},{20,28},{24,0},{28,4},{1,9},{5... | collective-permute-start | bytes 56 | tf_op jit(solution)/shard_map/ppermute | solution.py:175
  74.9 2.6 %collective-permute-start.2 = (s32[4]{0:T(128)S(1)}, s32[4]{0:T(128)S(1)}, u32[]{:S(2)}, u32[]{:S(2)}) collective-permute-start(s32[4]{0:T(128)S(1)} %get-tuple-element.10), channel_id=1, source_target_pairs={{0,12},{4,16},{8,20},{12,24},{16,28},{20,0},{24,4},{28,8},{1,13},{... | collective-permute-start | bytes 56 | tf_op jit(solution)/shard_map/ppermute | solution.py:175
  78.3 2.2 collective-permute-start.3
  81.6 3.7 %collective-permute-start.4 = (s32[4]{0:T(128)S(1)}, s32[4]{0:T(128)S(1)}, u32[]{:S(2)}, u32[]{:S(2)}) collective-permute-start(s32[4]{0:T(128)S(1)} %get-tuple-element.8), channel_id=1, source_target_pairs={{0,20},{4,24},{8,28},{12,0},{16,4},{20,8},{24,12},{28,16},{1,21},{... | collective-permute-start | bytes 56 | tf_op jit(solution)/shard_map/ppermute | solution.py:175
  91.3 2.9 %collective-permute-done.6 = s32[4]{0:T(128)S(1)} collective-permute-done((s32[4]{0:T(128)S(1)}, s32[4]{0:T(128)S(1)}, u32[]{:S(2)}, u32[]{:S(2)}) %collective-permute-start.6) | collective-permute-done | bytes 48 | tf_op jit(solution)/shard_map/ppermute | solution.py:175
  94.7 3.3 %collective-permute-start.28 = (f32[32,256]{1,0:T(8,128)S(1)}, f32[32,256]{1,0:T(8,128)S(1)}, u32[]{:S(2)}, u32[]{:S(2)}) collective-permute-start(f32[32,256]{1,0:T(8,128)S(1)} %bitcast.86), channel_id=1, source_target_pairs={{0,8},{4,12},{8,16},{12,20},{16,24},{20,28},{24,0},{28,4},{1,9},{5... | collective-permute-start | bytes 98312 | tf_op jit(solution)/shard_map/ppermute | solution.py:190
  109.5 19.3 %shard_map.95 = f32[32,128,256]{2,1,0:T(8,128)} custom-call(s32[640]{0:T(1024)S(1)} %get-tuple-element.33.rows_ref, s32[640]{0:T(1024)S(1)} %get-tuple-element.34.slots_ref, s32[1]{0:T(128)} %copy.39.cnt_ref, bf16[640,128,128]{2,1,0:T(8,128)(2,1)} %tv_ref.1, bf16[32,128,256]{2,1,0:T(8,128)(2,1)S(1)} %bitcast.76), custom_call_target="tpu_custom_call" | custom-call | tf_op jit(solution)/shard_map/pallas_call | solution.py:51
  128.8 3.3 %fusion.16 = (f32[4,128,256]{2,1,0:T(8,128)S(1)}, f32[4,128,256]{2,1,0:T(8,128)S(1)}, f32[4,128,256]{2,1,0:T(8,128)S(1)}, f32[4,128,256]{2,1,0:T(8,128)S(1)}, f3...) fusion(f32[32,128,256]{2,1,0:T(8,128)} %shard_map.95), kind=kLoop, calls=%fused_computation.102 | loop fusion | bytes 8388608 | tf_op jit(solution)/shard_map/slice | solution.py:176
  132.2 8.1 %collective-permute-start.12 = (f32[4,128,256]{2,1,0:T(8,128)S(1)}, f32[4,128,256]{2,1,0:T(8,128)S(1)}, u32[]{:S(2)}, u32[]{:S(2)}) collective-permute-start(f32[4,128,256]{2,1,0:T(8,128)S(1)} %get-tuple-element.20), channel_id=1, source_target_pairs={{0,12},{4,16},{8,20},{12,24},{16,28},{20,0},{24,4},{28,8},{1,13},{... | collective-permute-start | bytes 1572872 | tf_op jit(solution)/shard_map/ppermute | solution.py:175
  143.2 5.1 %collective-permute-start.15 = (f32[4,128,256]{2,1,0:T(8,128)S(1)}, f32[4,128,256]{2,1,0:T(8,128)S(1)}, u32[]{:S(2)}, u32[]{:S(2)}) collective-permute-start(f32[4,128,256]{2,1,0:T(8,128)S(1)} %get-tuple-element.17), channel_id=1, source_target_pairs={{0,24},{4,28},{8,0},{12,4},{16,8},{20,12},{24,16},{28,20},{1,25},{... | collective-permute-start | bytes 1572872 | tf_op jit(solution)/shard_map/ppermute | solution.py:175
  149.2 10.8 %collective-permute-done.11 = f32[4,128,256]{2,1,0:T(8,128)S(1)} collective-permute-done((f32[4,128,256]{2,1,0:T(8,128)S(1)}, f32[4,128,256]{2,1,0:T(8,128)S(1)}, u32[]{:S(2)}, u32[]{:S(2)}) %collective-permute-start.11) | collective-permute-done | bytes 524320 | tf_op jit(solution)/shard_map/ppermute | solution.py:175
  160.9 49.8 %collective-permute-done.12 = f32[4,128,256]{2,1,0:T(8,128)S(1)} collective-permute-done((f32[4,128,256]{2,1,0:T(8,128)S(1)}, f32[4,128,256]{2,1,0:T(8,128)S(1)}, u32[]{:S(2)}, u32[]{:S(2)}) %collective-permute-start.12) | collective-permute-done | bytes 524320 | tf_op jit(solution)/shard_map/ppermute | solution.py:175
  211.5 10.4 %collective-permute-done.13 = f32[4,128,256]{2,1,0:T(8,128)S(1)} collective-permute-done((f32[4,128,256]{2,1,0:T(8,128)S(1)}, f32[4,128,256]{2,1,0:T(8,128)S(1)}, u32[]{:S(2)}, u32[]{:S(2)}) %collective-permute-start.13) | collective-permute-done | bytes 524320 | tf_op jit(solution)/shard_map/ppermute | solution.py:175
  223.6 7.1 %collective-permute-done.15 = f32[4,128,256]{2,1,0:T(8,128)S(1)} collective-permute-done((f32[4,128,256]{2,1,0:T(8,128)S(1)}, f32[4,128,256]{2,1,0:T(8,128)S(1)}, u32[]{:S(2)}, u32[]{:S(2)}) %collective-permute-start.15) | collective-permute-done | bytes 524320 | tf_op jit(solution)/shard_map/ppermute | solution.py:175
  232.4 6.4 %shard_map.96 = f32[8,128,256]{2,1,0:T(8,128)} custom-call(s32[32]{0:T(128)} %concatenate.12.map_ref, f32[32,128,256]{2,1,0:T(8,128)} %constant_dynamic-update-slice_fusion.recv_ref), custom_call_target="tpu_custom_call" | custom-call | tf_op jit(solution)/shard_map/pallas_call | solution.py:93
  (106 shorter events, 47.7 us)
Async XLA Ops:
  2.3 107.1 %collective-permute-start.9 = (bf16[1024,256]{1,0:T(8,128)(2,1)S(1)}, bf16[1024,256]{1,0:T(8,128)(2,1)S(1)}, u32[]{:S(2)}, u32[]{:S(2)}) collective-permute-start(bf16[1024,256]{1,0:T(8,128)(2,1)S(1)} %convolution_convert_fusion), channel_id=1, source_target_pairs={{0,3},{1,0},{2,1},{3,2},{4,7},{5,4},{6,5},{7,6},{8,11},{9,8},{10,9... | collective-permute-start | bytes 1572872 | tf_op jit(solution)/shard_map/ppermute | solution.py:131
  4.5 104.9 %collective-permute-start.8 = (bf16[1024,256]{1,0:T(8,128)(2,1)S(1)}, bf16[1024,256]{1,0:T(8,128)(2,1)S(1)}, u32[]{:S(2)}, u32[]{:S(2)}) collective-permute-start(bf16[1024,256]{1,0:T(8,128)(2,1)S(1)} %convolution_convert_fusion), channel_id=1, source_target_pairs={{0,2},{1,3},{2,0},{3,1},{4,6},{5,7},{6,4},{7,5},{8,10},{9,11},{10,... | collective-permute-start | bytes 1572872 | tf_op jit(solution)/shard_map/ppermute | solution.py:131
  6.3 14.5 %collective-permute-start.19 = (f32[256,256]{1,0:T(8,128)S(1)}, f32[256,256]{1,0:T(8,128)S(1)}, u32[]{:S(2)}, u32[]{:S(2)}) collective-permute-start(f32[256,256]{1,0:T(8,128)S(1)} %bitcast.79), channel_id=1, source_target_pairs={{0,3},{1,0},{2,1},{3,2},{4,7},{5,4},{6,5},{7,6},{8,11},{9,8},{10,9... | collective-permute-start | bytes 786440 | tf_op jit(solution)/shard_map/ppermute | solution.py:131
  6.6 16.9 %collective-permute-start.18 = (f32[256,256]{1,0:T(8,128)S(1)}, f32[256,256]{1,0:T(8,128)S(1)}, u32[]{:S(2)}, u32[]{:S(2)}) collective-permute-start(f32[256,256]{1,0:T(8,128)S(1)} %bitcast.80), channel_id=1, source_target_pairs={{0,2},{1,3},{2,0},{3,1},{4,6},{5,7},{6,4},{7,5},{8,10},{9,11},{10,... | collective-permute-start | bytes 786440 | tf_op jit(solution)/shard_map/ppermute | solution.py:131
  7.8 34.7 %collective-permute-start.17 = (f32[256,256]{1,0:T(8,128)S(1)}, f32[256,256]{1,0:T(8,128)}, u32[]{:S(2)}, u32[]{:S(2)}) collective-permute-start(f32[256,256]{1,0:T(8,128)S(1)} %bitcast.81), channel_id=1, source_target_pairs={{0,1},{1,2},{2,3},{3,0},{4,5},{5,6},{6,7},{7,4},{8,9},{9,10},{10,1... | collective-permute-start | bytes 786440 | tf_op jit(solution)/shard_map/ppermute | solution.py:131
  20.8 88.6 %collective-permute-start.7 = (bf16[1024,256]{1,0:T(8,128)(2,1)S(1)}, bf16[1024,256]{1,0:T(8,128)(2,1)S(1)}, u32[]{:S(2)}, u32[]{:S(2)}) collective-permute-start(bf16[1024,256]{1,0:T(8,128)(2,1)S(1)} %convolution_convert_fusion), channel_id=1, source_target_pairs={{0,1},{1,2},{2,3},{3,0},{4,5},{5,6},{6,7},{7,4},{8,9},{9,10},{10,1... | collective-permute-start | bytes 1572872 | tf_op jit(solution)/shard_map/ppermute | solution.py:131
  23.5 47.2 %collective-permute-start = (s32[4]{0:T(128)S(1)}, s32[4]{0:T(128)S(1)}, u32[]{:S(2)}, u32[]{:S(2)}) collective-permute-start(s32[4]{0:T(128)S(1)} %get-tuple-element.12), channel_id=1, source_target_pairs={{0,4},{4,8},{8,12},{12,16},{16,20},{20,24},{24,28},{28,0},{1,5},{5... | collective-permute-start | bytes 56 | tf_op jit(solution)/shard_map/ppermute | solution.py:175
  47.7 7.4 %collective-permute-start.22 = (f32[32,256]{1,0:T(8,128)S(1)}, f32[32,256]{1,0:T(8,128)S(1)}, u32[]{:S(2)}, u32[]{:S(2)}) collective-permute-start(f32[32,256]{1,0:T(8,128)S(1)} %get-tuple-element.28), channel_id=1, source_target_pairs={{0,12},{4,16},{8,20},{12,24},{16,28},{20,0},{24,4},{28,8},{1,13},{... | collective-permute-start | bytes 98312 | tf_op jit(solution)/shard_map/ppermute | solution.py:175
  55.0 4.3 %collective-permute-start.23 = (f32[32,256]{1,0:T(8,128)S(1)}, f32[32,256]{1,0:T(8,128)S(1)}, u32[]{:S(2)}, u32[]{:S(2)}) collective-permute-start(f32[32,256]{1,0:T(8,128)S(1)} %get-tuple-element.27), channel_id=1, source_target_pairs={{0,16},{4,20},{8,24},{12,28},{16,0},{20,4},{24,8},{28,12},{1,17},{... | collective-permute-start | bytes 98312 | tf_op jit(solution)/shard_map/ppermute | solution.py:175
  59.3 4.6 %collective-permute-start.24 = (f32[32,256]{1,0:T(8,128)S(1)}, f32[32,256]{1,0:T(8,128)S(1)}, u32[]{:S(2)}, u32[]{:S(2)}) collective-permute-start(f32[32,256]{1,0:T(8,128)S(1)} %get-tuple-element.26), channel_id=1, source_target_pairs={{0,20},{4,24},{8,28},{12,0},{16,4},{20,8},{24,12},{28,16},{1,21},{... | collective-permute-start | bytes 98312 | tf_op jit(solution)/shard_map/ppermute | solution.py:175
  70.6 27.4 %collective-permute-start.27 = (f32[32,256]{1,0:T(8,128)S(1)}, f32[32,256]{1,0:T(8,128)S(1)}, u32[]{:S(2)}, u32[]{:S(2)}) collective-permute-start(f32[32,256]{1,0:T(8,128)S(1)} %bitcast.85), channel_id=1, source_target_pairs={{0,4},{4,8},{8,12},{12,16},{16,20},{20,24},{24,28},{28,0},{1,5},{5... | collective-permute-start | bytes 98312 | tf_op jit(solution)/shard_map/ppermute | solution.py:190
  70.7 4.2 %collective-permute-start.1 = (s32[4]{0:T(128)S(1)}, s32[4]{0:T(128)S(1)}, u32[]{:S(2)}, u32[]{:S(2)}) collective-permute-start(s32[4]{0:T(128)S(1)} %get-tuple-element.11), channel_id=1, source_target_pairs={{0,8},{4,12},{8,16},{12,20},{16,24},{20,28},{24,0},{28,4},{1,9},{5... | collective-permute-start | bytes 56 | tf_op jit(solution)/shard_map/ppermute | solution.py:175
  81.6 5.5 %collective-permute-start.4 = (s32[4]{0:T(128)S(1)}, s32[4]{0:T(128)S(1)}, u32[]{:S(2)}, u32[]{:S(2)}) collective-permute-start(s32[4]{0:T(128)S(1)} %get-tuple-element.8), channel_id=1, source_target_pairs={{0,20},{4,24},{8,28},{12,0},{16,4},{20,8},{24,12},{28,16},{1,21},{... | collective-permute-start | bytes 56 | tf_op jit(solution)/shard_map/ppermute | solution.py:175
  89.5 4.6 %collective-permute-start.6 = (s32[4]{0:T(128)S(1)}, s32[4]{0:T(128)S(1)}, u32[]{:S(2)}, u32[]{:S(2)}) collective-permute-start(s32[4]{0:T(128)S(1)} %get-tuple-element.6), channel_id=1, source_target_pairs={{0,28},{4,0},{8,4},{12,8},{16,12},{20,16},{24,20},{28,24},{1,29},{... | collective-permute-start | bytes 56 | tf_op jit(solution)/shard_map/ppermute | solution.py:175
  94.7 4.3 %collective-permute-start.28 = (f32[32,256]{1,0:T(8,128)S(1)}, f32[32,256]{1,0:T(8,128)S(1)}, u32[]{:S(2)}, u32[]{:S(2)}) collective-permute-start(f32[32,256]{1,0:T(8,128)S(1)} %bitcast.86), channel_id=1, source_target_pairs={{0,8},{4,12},{8,16},{12,20},{16,24},{20,28},{24,0},{28,4},{1,9},{5... | collective-permute-start | bytes 98312 | tf_op jit(solution)/shard_map/ppermute | solution.py:190
  101.4 4.6 %collective-permute-start.31 = (f32[32,256]{1,0:T(8,128)S(1)}, f32[32,256]{1,0:T(8,128)S(1)}, u32[]{:S(2)}, u32[]{:S(2)}) collective-permute-start(f32[32,256]{1,0:T(8,128)S(1)} %bitcast.89), channel_id=1, source_target_pairs={{0,20},{4,24},{8,28},{12,0},{16,4},{20,8},{24,12},{28,16},{1,21},{... | collective-permute-start | bytes 98312 | tf_op jit(solution)/shard_map/ppermute | solution.py:190
  102.8 4.4 %collective-permute-start.32 = (f32[32,256]{1,0:T(8,128)S(1)}, f32[32,256]{1,0:T(8,128)S(1)}, u32[]{:S(2)}, u32[]{:S(2)}) collective-permute-start(f32[32,256]{1,0:T(8,128)S(1)} %bitcast.90), channel_id=1, source_target_pairs={{0,24},{4,28},{8,0},{12,4},{16,8},{20,12},{24,16},{28,20},{1,25},{... | collective-permute-start | bytes 98312 | tf_op jit(solution)/shard_map/ppermute | solution.py:190
  132.1 11.1 %collective-permute-start.10 = (f32[4,128,256]{2,1,0:T(8,128)S(1)}, f32[4,128,256]{2,1,0:T(8,128)S(1)}, u32[]{:S(2)}, u32[]{:S(2)}) collective-permute-start(f32[4,128,256]{2,1,0:T(8,128)S(1)} %get-tuple-element.22), channel_id=1, source_target_pairs={{0,4},{4,8},{8,12},{12,16},{16,20},{20,24},{24,28},{28,0},{1,5},{5... | collective-permute-start | bytes 1572872 | tf_op jit(solution)/shard_map/ppermute | solution.py:175
  132.1 27.9 %collective-permute-start.11 = (f32[4,128,256]{2,1,0:T(8,128)S(1)}, f32[4,128,256]{2,1,0:T(8,128)S(1)}, u32[]{:S(2)}, u32[]{:S(2)}) collective-permute-start(f32[4,128,256]{2,1,0:T(8,128)S(1)} %get-tuple-element.21), channel_id=1, source_target_pairs={{0,8},{4,12},{8,16},{12,20},{16,24},{20,28},{24,0},{28,4},{1,9},{5... | collective-permute-start | bytes 1572872 | tf_op jit(solution)/shard_map/ppermute | solution.py:175
  132.2 78.5 %collective-permute-start.12 = (f32[4,128,256]{2,1,0:T(8,128)S(1)}, f32[4,128,256]{2,1,0:T(8,128)S(1)}, u32[]{:S(2)}, u32[]{:S(2)}) collective-permute-start(f32[4,128,256]{2,1,0:T(8,128)S(1)} %get-tuple-element.20), channel_id=1, source_target_pairs={{0,12},{4,16},{8,20},{12,24},{16,28},{20,0},{24,4},{28,8},{1,13},{... | collective-permute-start | bytes 1572872 | tf_op jit(solution)/shard_map/ppermute | solution.py:175
  140.4 81.6 %collective-permute-start.13 = (f32[4,128,256]{2,1,0:T(8,128)S(1)}, f32[4,128,256]{2,1,0:T(8,128)S(1)}, u32[]{:S(2)}, u32[]{:S(2)}) collective-permute-start(f32[4,128,256]{2,1,0:T(8,128)S(1)} %get-tuple-element.19), channel_id=1, source_target_pairs={{0,16},{4,20},{8,24},{12,28},{16,0},{20,4},{24,8},{28,12},{1,17},{... | collective-permute-start | bytes 1572872 | tf_op jit(solution)/shard_map/ppermute | solution.py:175
  140.4 82.4 %collective-permute-start.14 = (f32[4,128,256]{2,1,0:T(8,128)S(1)}, f32[4,128,256]{2,1,0:T(8,128)S(1)}, u32[]{:S(2)}, u32[]{:S(2)}) collective-permute-start(f32[4,128,256]{2,1,0:T(8,128)S(1)} %get-tuple-element.18), channel_id=1, source_target_pairs={{0,20},{4,24},{8,28},{12,0},{16,4},{20,8},{24,12},{28,16},{1,21},{... | collective-permute-start | bytes 1572872 | tf_op jit(solution)/shard_map/ppermute | solution.py:175
  143.2 87.4 %collective-permute-start.15 = (f32[4,128,256]{2,1,0:T(8,128)S(1)}, f32[4,128,256]{2,1,0:T(8,128)S(1)}, u32[]{:S(2)}, u32[]{:S(2)}) collective-permute-start(f32[4,128,256]{2,1,0:T(8,128)S(1)} %get-tuple-element.17), channel_id=1, source_target_pairs={{0,24},{4,28},{8,0},{12,4},{16,8},{20,12},{24,16},{28,20},{1,25},{... | collective-permute-start | bytes 1572872 | tf_op jit(solution)/shard_map/ppermute | solution.py:175
  160.0 71.5 %collective-permute-start.16 = (f32[4,128,256]{2,1,0:T(8,128)S(1)}, f32[4,128,256]{2,1,0:T(8,128)S(1)}, u32[]{:S(2)}, u32[]{:S(2)}) collective-permute-start(f32[4,128,256]{2,1,0:T(8,128)S(1)} %get-tuple-element.16), channel_id=1, source_target_pairs={{0,28},{4,0},{8,4},{12,8},{16,12},{20,16},{24,20},{28,24},{1,29},{... | collective-permute-start | bytes 1572872 | tf_op jit(solution)/shard_map/ppermute | solution.py:175
  (13 other events, 173.9 us)
where the time goes:
time: 239 us
  waiting for transfers between devices  118 us (49%)
  starting transfers between devices  76.4 us (32%)
  Pallas kernels  25.7 us (11%)
  local copies, waits for them, and re-layouts  10.4 us (4%)
  matrix products  3.14 us (1%)
  other arithmetic  2.79 us (1%)
    ppermute x21, waiting for transfers between devices, shards(): lax.ppermute((compact[shift * CAP:(shift + 1) * CAP], table[shift], _pick...  103 us
    ppermute x21, starting transfers between devices, shards(): lax.ppermute((compact[shift * CAP:(shift + 1) * CAP], table[shift], _pick...  59.9 us
    pallas_call x1, Pallas kernels, _spmm(): pl.pallas_call(_spmm_kernel, out_shape=jax.ShapeDtypeStruct((out_blocks,...  19.3 us
    ppermute x6, waiting for transfers between devices, shards(): piece, term = lax.ppermute((projected, weight_term), 'loop', pairs)  9.63 us
    ppermute x7, starting transfers between devices, shards(): gathered.append(lax.ppermute(own, 'dom', pairs))  9.12 us
    ppermute x6, starting transfers between devices, shards(): piece, term = lax.ppermute((projected, weight_term), 'loop', pairs)  7.35 us
    pallas_call x1, Pallas kernels, _combine(): pl.pallas_call(_combine_kernel, out_shape=jax.ShapeDtypeStruct((out_block...  6.38 us
    ppermute x7, waiting for transfers between devices, shards(): gathered.append(lax.ppermute(own, 'dom', pairs))  5.48 us
  transfers between devices with their start and end apart: 34, of which 25 were waited for; matrix products, arithmetic and copies ran while one was open for 4% of the time, Pallas kernels for 0%

commit v1 on v0

--- a/solution.py
+++ b/solution.py
@@ -11,15 +11,19 @@
 CAP = 4
 
 
-def _spmm_kernel(rows_ref, slots_ref, cnt_ref, tv_ref, part_ref, out_ref):
+def _spmm_kernel(rows_ref, slots_ref, cnt_ref, tv_ref, part_ref, extra_ref, out_ref):
     g = pl.program_id(0)
     count = cnt_ref[0]
-    group = tv_ref.shape[0]
+    group, tile_size, _ = tv_ref.shape
     base = g * group
+    body_rows = CAP * tile_size
 
     @pl.when(g == 0)
     def _():
-        out_ref[...] = jnp.zeros(out_ref.shape, out_ref.dtype)
+        out_ref[:, :body_rows, :] = jnp.zeros(
+            (out_ref.shape[0], body_rows, out_ref.shape[2]), out_ref.dtype
+        )
+        out_ref[:, body_rows:, :] = extra_ref[...]
 
     @pl.when(base < count)
     def _():
@@ -33,12 +37,17 @@
                 (((0,), (0,)), ((), ())),
                 preferred_element_type=jnp.float32,
             )
-            out_ref[c] += jnp.where(j < count, term, 0.0)
-
-
-def _spmm(rows, slots, count, tile_values, partition, out_blocks):
+            dest = c // CAP
+            start = pl.multiple_of((c % CAP) * tile_size, tile_size)
+            window = out_ref.at[dest, pl.ds(start, tile_size), :]
+            window[...] += jnp.where(j < count, term, 0.0)
+
+
+def _spmm(rows, slots, count, tile_values, partition, extra):
     tiles, tile_size, _ = tile_values.shape
     part_blocks, _, width = partition.shape
+    dests, extra_rows, _ = extra.shape
+    out_rows = CAP * tile_size + extra_rows
     group = math.gcd(tiles, GROUP)
 
     def tv_map(g, rows_ref, slots_ref, cnt_ref):
@@ -50,39 +59,44 @@
 
     return pl.pallas_call(
         _spmm_kernel,
-        out_shape=jax.ShapeDtypeStruct((out_blocks, tile_size, width), jnp.float32),
+        out_shape=jax.ShapeDtypeStruct((dests, out_rows, width), jnp.float32),
         grid_spec=pltpu.PrefetchScalarGridSpec(
             num_scalar_prefetch=3,
             grid=(tiles // group,),
             in_specs=[
                 pl.BlockSpec((group, tile_size, tile_size), tv_map),
                 pl.BlockSpec((part_blocks, tile_size, width), whole),
+                pl.BlockSpec((dests, extra_rows, width), whole),
             ],
-            out_specs=pl.BlockSpec((out_blocks, tile_size, width), whole),
+            out_specs=pl.BlockSpec((dests, out_rows, width), whole),
         ),
         compiler_params=pltpu.CompilerParams(
             dimension_semantics=("arbitrary",),
             vmem_limit_bytes=50 * 1024 * 1024,
         ),
-    )(rows, slots, count, tile_values, partition)
+        cost_estimate=pl.CostEstimate(
+            flops=2 * tiles * tile_size * tile_size * width,
+            transcendentals=0,
+            bytes_accessed=tiles * tile_size * tile_size * 2 + dests * out_rows * width * 4,
+        ),
+    )(rows, slots, count, tile_values, partition, extra)
 
 
 def _combine_kernel(map_ref, recv_ref, out_ref):
     g = pl.program_id(0)
-    per = recv_ref.shape[0]
+    tile_size = out_ref.shape[1]
 
     @pl.when(g == 0)
     def _():
         out_ref[...] = jnp.zeros(out_ref.shape, out_ref.dtype)
 
-    for k in range(per):
-        b = map_ref[g * per + k]
-        out_ref[b] += recv_ref[k]
-
-
-def _combine(block_map, received, out_blocks):
-    total, tile_size, width = received.shape
-    per = CAP
+    for k in range(CAP):
+        b = map_ref[g * CAP + k]
+        out_ref[b] += recv_ref[0, k * tile_size:(k + 1) * tile_size, :]
+
+
+def _combine(block_map, received, out_blocks, tile_size):
+    total, _, width = received.shape
 
     def recv_map(g, map_ref):
         return (g, 0, 0)
@@ -95,11 +109,16 @@
         out_shape=jax.ShapeDtypeStruct((out_blocks, tile_size, width), jnp.float32),
         grid_spec=pltpu.PrefetchScalarGridSpec(
             num_scalar_prefetch=1,
-            grid=(total // per,),
-            in_specs=[pl.BlockSpec((per, tile_size, width), recv_map)],
+            grid=(total,),
+            in_specs=[pl.BlockSpec((1, CAP * tile_size, width), recv_map)],
             out_specs=pl.BlockSpec((out_blocks, tile_size, width), whole),
         ),
         compiler_params=pltpu.CompilerParams(dimension_semantics=("arbitrary",)),
+        cost_estimate=pl.CostEstimate(
+            flops=total * CAP * tile_size * width,
+            transcendentals=0,
+            bytes_accessed=(total * CAP + out_blocks) * tile_size * width * 4,
+        ),
     )(block_map, received)
 
 
@@ -163,24 +182,23 @@
     dest_dom = cols // local_blocks
     slots = ((dest_dom - dom_index) % dom_count) * CAP + tile_rank
 
-    compact = _spmm(rows, slots, tile_counts, tile_values, partition, dom_count * CAP)
-
     chunk = width // dom_count
     chunks = loop_sum.reshape(dom_count, chunk, width)
-    received = [compact[:CAP]]
-    maps = [table[0]]
-    parts = [_pick(chunks, dom_index)]
+    chunks = jnp.stack([_pick(chunks, (dom_index + shift) % dom_count) for shift in range(dom_count)])
+    id_rows = jnp.zeros((dom_count, 8, width), jnp.float32)
+    id_rows = id_rows.at[:, 0, :CAP].set(table.astype(jnp.float32))
+    extra = jnp.concatenate([chunks, id_rows], axis=1)
+
+    compact = _spmm(rows, slots, tile_counts, tile_values, partition, extra)
+
+    received = [compact[0]]
     for shift in range(1, dom_count):
         pairs = [(i, (i + shift) % dom_count) for i in range(dom_count)]
-        slab, ids, part = lax.ppermute(
-            (compact[shift * CAP:(shift + 1) * CAP], table[shift], _pick(chunks, (dom_index + shift) % dom_count)),
-            "dom",
-            pairs,
-        )
-        received.append(slab)
-        maps.append(ids)
-        parts.append(part)
-    parts = jnp.stack(parts)
+        received.append(lax.ppermute(compact[shift], "dom", pairs))
+    received = jnp.stack(received)
+    body_rows = CAP * tile_size
+    parts = received[:, body_rows:body_rows + chunk, :]
+    block_map = received[:, body_rows + chunk, :CAP].astype(jnp.int32).reshape(-1)
     own = _pick(parts, dom_index % dom_count)
     for source in range(1, dom_count):
         own = own + _pick(parts, (dom_index - source) % dom_count)
@@ -192,9 +210,7 @@
     weight_grad = jnp.concatenate(
         [_pick(gathered, (dom_index - k) % dom_count) for k in range(dom_count)], axis=0
     )
-    node_grad = _combine(
-        jnp.concatenate(maps), jnp.concatenate(received, axis=0), local_blocks
-    ).reshape(node_rows, width)
+    node_grad = _combine(block_map, received, local_blocks, tile_size).reshape(node_rows, width)
     return (node_grad, weight_grad)
 
 

time: 239 us -> 186 us (0.78)
  the two profiles are of different devices: /device:TPU:9 before, /device:TPU:31 now
where the time goes in v1:
time: 186 us; the launch traced here: 183 us
  waiting for transfers between devices  107 us (58%)
  starting transfers between devices  38.9 us (21%)
  Pallas kernels  15.1 us (8%)
  local copies, waits for them, and re-layouts  13.7 us (7%)
  other arithmetic  3.33 us (2%)
  matrix products  3.09 us (2%)
    ppermute x7, waiting for transfers between devices, shards(): received.append(lax.ppermute(compact[shift], 'dom', pairs))  76.9 us
    ppermute x6, waiting for transfers between devices, shards(): piece, term = lax.ppermute((projected, weight_term), 'loop', pairs)  25.5 us
    ppermute x7, starting transfers between devices, shards(): received.append(lax.ppermute(compact[shift], 'dom', pairs))  22.1 us
    ppermute x7, starting transfers between devices, shards(): gathered.append(lax.ppermute(own, 'dom', pairs))  12.2 us
    pallas_call x1, Pallas kernels, _spmm(): pl.pallas_call(_spmm_kernel, out_shape=jax.ShapeDtypeStruct((dests, out_r...  8.74 us
    unnamed x30, local copies, waits for them, and re-layouts  7 us
    pallas_call x1, Pallas kernels, _combine(): pl.pallas_call(_combine_kernel, out_shape=jax.ShapeDtypeStruct((out_block...  6.38 us
    ppermute x6, starting transfers between devices, shards(): piece, term = lax.ppermute((projected, weight_term), 'loop', pairs)  4.55 us
  transfers between devices with their start and end apart: 20, of which 9 were waited for; matrix products, arithmetic and copies ran while one was open for 6% of the time, Pallas kernels for 3%

profile of v1, /device:TPU:31, one launch (start us, length us, event | category | flops | bytes accessed | tf_op | source)
XLA Modules:
  0.0 182.7 jit_solution(18184531018783395249)
XLA Ops:
  0.6 1.0 copy-done
  1.7 1.5 convolution_multiply_fusion
  3.5 1.2 collective-permute-start.4
  5.0 1.5 convolution_convert_fusion
  6.5 2.2 %collective-permute-start = (bf16[1024,256]{1,0:T(8,128)(2,1)S(1)}, bf16[1024,256]{1,0:T(8,128)(2,1)S(1)}, u32[]{:S(2)}, u32[]{:S(2)}) collective-permute-start(bf16[1024,256]{1,0:T(8,128)(2,1)S(1)} %convolution_convert_fusion), channel_id=1, source_target_pairs={{0,1},{1,2},{2,3},{3,0},{4,5},{5,6},{6,7},{7,4},{8,9},{9,10},{10,1... | collective-permute-start | bytes 1572872 | tf_op jit(solution)/shard_map/ppermute | solution.py:150
  12.8 3.3 %collective-permute-done.5 = f32[256,256]{1,0:T(8,128)S(1)} collective-permute-done((f32[256,256]{1,0:T(8,128)S(1)}, f32[256,256]{1,0:T(8,128)S(1)}, u32[]{:S(2)}, u32[]{:S(2)}) %collective-permute-start.5) | collective-permute-done | bytes 262176 | tf_op jit(solution)/shard_map/ppermute | solution.py:150
  16.4 10.9 %collective-permute-done = bf16[1024,256]{1,0:T(8,128)(2,1)S(1)} collective-permute-done((bf16[1024,256]{1,0:T(8,128)(2,1)S(1)}, bf16[1024,256]{1,0:T(8,128)(2,1)S(1)}, u32[]{:S(2)}, u32[]{:S(2)}) %collective-permute-start) | collective-permute-done | bytes 524320 | tf_op jit(solution)/shard_map/ppermute | solution.py:150
  27.4 1.0 collective-permute-done.1
  28.3 10.2 %collective-permute-done.2 = bf16[1024,256]{1,0:T(8,128)(2,1)S(1)} collective-permute-done((bf16[1024,256]{1,0:T(8,128)(2,1)S(1)}, bf16[1024,256]{1,0:T(8,128)(2,1)S(1)}, u32[]{:S(2)}, u32[]{:S(2)}) %collective-permute-start.2) | collective-permute-done | bytes 524320 | tf_op jit(solution)/shard_map/ppermute | solution.py:150
  38.7 8.7 %shard_map.95 = f32[8,552,256]{2,1,0:T(8,128)} custom-call(s32[640]{0:T(1024)S(1)} %get-tuple-element.29.rows_ref, s32[640]{0:T(1024)S(1)} %get-tuple-element.30.slots_ref, s32[1]{0:T(128)} %copy.43.cnt_ref, bf16[640,128,128]{2,1,0:T(8,128)(2,1)} %tv_ref.1, bf16[32,128,256]{2,1,0:T(8,128)(2,1)S(1)} %bitcast.78, f32[8,40,256]{2,1,0:T(8,128)S(1)} %select_maximum_fusion.extra_ref), custom_call_target="tpu_custom_call" | custom-call | flops 5368709120 | bytes 25493504 | tf_op jit(solution)/shard_map/pallas_call | solution.py:60
  47.5 4.0 %slice_bitcast_fusion = (f32[552,256]{1,0:T(8,128)S(1)}, f32[552,256]{1,0:T(8,128)S(1)}, f32[552,256]{1,0:T(8,128)}, f32[552,256]{1,0:T(8,128)}, f32[552,256]{1,...) fusion(f32[8,552,256]{2,1,0:T(8,128)} %shard_map.95), kind=kLoop, calls=%fused_computation.5 | loop fusion | bytes 9043968 | tf_op jit(solution)/shard_map/squeeze | solution.py:197
  51.5 4.5 %collective-permute-start.6 = (f32[552,256]{1,0:T(8,128)}, f32[552,256]{1,0:T(8,128)S(1)}, u32[]{:S(2)}, u32[]{:S(2)}) collective-permute-start(f32[552,256]{1,0:T(8,128)} %get-tuple-element.26), channel_id=1, source_target_pairs={{0,4},{4,8},{8,12},{12,16},{16,20},{20,24},{24,28},{28,0},{1,5},{5... | collective-permute-start | bytes 1695752 | tf_op jit(solution)/shard_map/ppermute | solution.py:197
  56.0 11.6 %collective-permute-start.7 = (f32[552,256]{1,0:T(8,128)}, f32[552,256]{1,0:T(8,128)S(1)}, u32[]{:S(2)}, u32[]{:S(2)}) collective-permute-start(f32[552,256]{1,0:T(8,128)} %get-tuple-element.25), channel_id=1, source_target_pairs={{0,8},{4,12},{8,16},{12,20},{16,24},{20,28},{24,0},{28,4},{1,9},{5... | collective-permute-start | bytes 1695752 | tf_op jit(solution)/shard_map/ppermute | solution.py:197
  67.6 3.0 %collective-permute-start.9 = (f32[552,256]{1,0:T(8,128)}, f32[552,256]{1,0:T(8,128)S(1)}, u32[]{:S(2)}, u32[]{:S(2)}) collective-permute-start(f32[552,256]{1,0:T(8,128)} %get-tuple-element.23), channel_id=1, source_target_pairs={{0,16},{4,20},{8,24},{12,28},{16,0},{20,4},{24,8},{28,12},{1,17},{... | collective-permute-start | bytes 1695752 | tf_op jit(solution)/shard_map/ppermute | solution.py:197
  72.1 7.6 %collective-permute-done.7 = f32[552,256]{1,0:T(8,128)S(1)} collective-permute-done((f32[552,256]{1,0:T(8,128)}, f32[552,256]{1,0:T(8,128)S(1)}, u32[]{:S(2)}, u32[]{:S(2)}) %collective-permute-start.7) | collective-permute-done | bytes 565280 | tf_op jit(solution)/shard_map/ppermute | solution.py:197
  79.7 2.3 %collective-permute-start.12 = (f32[552,256]{1,0:T(8,128)S(1)}, f32[552,256]{1,0:T(8,128)S(1)}, u32[]{:S(2)}, u32[]{:S(2)}) collective-permute-start(f32[552,256]{1,0:T(8,128)S(1)} %get-tuple-element.20), channel_id=1, source_target_pairs={{0,28},{4,0},{8,4},{12,8},{16,12},{20,16},{24,20},{28,24},{1,29},{... | collective-permute-start | bytes 1695752 | tf_op jit(solution)/shard_map/ppermute | solution.py:197
  82.8 9.0 %collective-permute-done.8 = f32[552,256]{1,0:T(8,128)S(1)} collective-permute-done((f32[552,256]{1,0:T(8,128)}, f32[552,256]{1,0:T(8,128)S(1)}, u32[]{:S(2)}, u32[]{:S(2)}) %collective-permute-start.8) | collective-permute-done | bytes 565280 | tf_op jit(solution)/shard_map/ppermute | solution.py:197
  92.6 60.4 %collective-permute-done.9 = f32[552,256]{1,0:T(8,128)S(1)} collective-permute-done((f32[552,256]{1,0:T(8,128)}, f32[552,256]{1,0:T(8,128)S(1)}, u32[]{:S(2)}, u32[]{:S(2)}) %collective-permute-start.9) | collective-permute-done | bytes 565280 | tf_op jit(solution)/shard_map/ppermute | solution.py:197
  158.4 6.5 %collective-permute-start.15 = (f32[32,256]{1,0:T(8,128)S(1)}, f32[32,256]{1,0:T(8,128)S(1)}, u32[]{:S(2)}, u32[]{:S(2)}) collective-permute-start(f32[32,256]{1,0:T(8,128)S(1)} %bitcast.97), channel_id=1, source_target_pairs={{0,12},{4,16},{8,20},{12,24},{16,28},{20,0},{24,4},{28,8},{1,13},{... | collective-permute-start | bytes 98312 | tf_op jit(solution)/shard_map/ppermute | solution.py:208
  164.9 2.1 %collective-permute-start.17 = (f32[32,256]{1,0:T(8,128)S(1)}, f32[32,256]{1,0:T(8,128)S(1)}, u32[]{:S(2)}, u32[]{:S(2)}) collective-permute-start(f32[32,256]{1,0:T(8,128)S(1)} %bitcast.99), channel_id=1, source_target_pairs={{0,20},{4,24},{8,28},{12,0},{16,4},{20,8},{24,12},{28,16},{1,21},{... | collective-permute-start | bytes 98312 | tf_op jit(solution)/shard_map/ppermute | solution.py:208
  168.3 6.4 %shard_map.96 = f32[8,128,256]{2,1,0:T(8,128)} custom-call(s32[32]{0:T(128)} %convert_element_type.33.map_ref, f32[8,552,256]{2,1,0:T(8,128)} %bitcast_dynamic-update-slice_fusion.recv_ref), custom_call_target="tpu_custom_call" | custom-call | flops 1048576 | bytes 5242880 | tf_op jit(solution)/shard_map/pallas_call | solution.py:107
  174.7 2.0 %collective-permute-start.18 = (f32[32,256]{1,0:T(8,128)S(1)}, f32[32,256]{1,0:T(8,128)S(1)}, u32[]{:S(2)}, u32[]{:S(2)}) collective-permute-start(f32[32,256]{1,0:T(8,128)S(1)} %bitcast.100), channel_id=1, source_target_pairs={{0,24},{4,28},{8,0},{12,4},{16,8},{20,12},{24,16},{28,20},{1,25},{... | collective-permute-start | bytes 98312 | tf_op jit(solution)/shard_map/ppermute | solution.py:208
  177.5 1.8 collective-permute-done.18
  179.3 2.6 %collective-permute-done.19 = f32[32,256]{1,0:T(8,128)S(1)} collective-permute-done((f32[32,256]{1,0:T(8,128)S(1)}, f32[32,256]{1,0:T(8,128)S(1)}, u32[]{:S(2)}, u32[]{:S(2)}) %collective-permute-start.19) | collective-permute-done | bytes 32800 | tf_op jit(solution)/shard_map/ppermute | solution.py:208
  (80 shorter events, 15.4 us)
Async XLA Ops:
  0.6 1.0 copy-start
  3.2 9.1 %collective-permute-start.3 = (f32[256,256]{1,0:T(8,128)S(1)}, f32[256,256]{1,0:T(8,128)S(1)}, u32[]{:S(2)}, u32[]{:S(2)}) collective-permute-start(f32[256,256]{1,0:T(8,128)S(1)} %bitcast.88), channel_id=1, source_target_pairs={{0,1},{1,2},{2,3},{3,0},{4,5},{5,6},{6,7},{7,4},{8,9},{9,10},{10,1... | collective-permute-start | bytes 786440 | tf_op jit(solution)/shard_map/ppermute | solution.py:150
  3.5 9.3 %collective-permute-start.4 = (f32[256,256]{1,0:T(8,128)S(1)}, f32[256,256]{1,0:T(8,128)S(1)}, u32[]{:S(2)}, u32[]{:S(2)}) collective-permute-start(f32[256,256]{1,0:T(8,128)S(1)} %bitcast.89), channel_id=1, source_target_pairs={{0,2},{1,3},{2,0},{3,1},{4,6},{5,7},{6,4},{7,5},{8,10},{9,11},{10,... | collective-permute-start | bytes 786440 | tf_op jit(solution)/shard_map/ppermute | solution.py:150
  4.7 11.3 %collective-permute-start.5 = (f32[256,256]{1,0:T(8,128)S(1)}, f32[256,256]{1,0:T(8,128)S(1)}, u32[]{:S(2)}, u32[]{:S(2)}) collective-permute-start(f32[256,256]{1,0:T(8,128)S(1)} %bitcast.90), channel_id=1, source_target_pairs={{0,3},{1,0},{2,1},{3,2},{4,7},{5,4},{6,5},{7,6},{8,11},{9,8},{10,9... | collective-permute-start | bytes 786440 | tf_op jit(solution)/shard_map/ppermute | solution.py:150
  6.5 20.8 %collective-permute-start = (bf16[1024,256]{1,0:T(8,128)(2,1)S(1)}, bf16[1024,256]{1,0:T(8,128)(2,1)S(1)}, u32[]{:S(2)}, u32[]{:S(2)}) collective-permute-start(bf16[1024,256]{1,0:T(8,128)(2,1)S(1)} %convolution_convert_fusion), channel_id=1, source_target_pairs={{0,1},{1,2},{2,3},{3,0},{4,5},{5,6},{6,7},{7,4},{8,9},{9,10},{10,1... | collective-permute-start | bytes 1572872 | tf_op jit(solution)/shard_map/ppermute | solution.py:150
  8.7 19.6 %collective-permute-start.1 = (bf16[1024,256]{1,0:T(8,128)(2,1)S(1)}, bf16[1024,256]{1,0:T(8,128)(2,1)S(1)}, u32[]{:S(2)}, u32[]{:S(2)}) collective-permute-start(bf16[1024,256]{1,0:T(8,128)(2,1)S(1)} %convolution_convert_fusion), channel_id=1, source_target_pairs={{0,2},{1,3},{2,0},{3,1},{4,6},{5,7},{6,4},{7,5},{8,10},{9,11},{10,... | collective-permute-start | bytes 1572872 | tf_op jit(solution)/shard_map/ppermute | solution.py:150
  12.3 26.2 %collective-permute-start.2 = (bf16[1024,256]{1,0:T(8,128)(2,1)S(1)}, bf16[1024,256]{1,0:T(8,128)(2,1)S(1)}, u32[]{:S(2)}, u32[]{:S(2)}) collective-permute-start(bf16[1024,256]{1,0:T(8,128)(2,1)S(1)} %convolution_convert_fusion), channel_id=1, source_target_pairs={{0,3},{1,0},{2,1},{3,2},{4,7},{5,4},{6,5},{7,6},{8,11},{9,8},{10,9... | collective-permute-start | bytes 1572872 | tf_op jit(solution)/shard_map/ppermute | solution.py:150
  51.5 19.2 %collective-permute-start.6 = (f32[552,256]{1,0:T(8,128)}, f32[552,256]{1,0:T(8,128)S(1)}, u32[]{:S(2)}, u32[]{:S(2)}) collective-permute-start(f32[552,256]{1,0:T(8,128)} %get-tuple-element.26), channel_id=1, source_target_pairs={{0,4},{4,8},{8,12},{12,16},{16,20},{20,24},{24,28},{28,0},{1,5},{5... | collective-permute-start | bytes 1695752 | tf_op jit(solution)/shard_map/ppermute | solution.py:197
  56.0 23.7 %collective-permute-start.7 = (f32[552,256]{1,0:T(8,128)}, f32[552,256]{1,0:T(8,128)S(1)}, u32[]{:S(2)}, u32[]{:S(2)}) collective-permute-start(f32[552,256]{1,0:T(8,128)} %get-tuple-element.25), channel_id=1, source_target_pairs={{0,8},{4,12},{8,16},{12,20},{16,24},{20,28},{24,0},{28,4},{1,9},{5... | collective-permute-start | bytes 1695752 | tf_op jit(solution)/shard_map/ppermute | solution.py:197
  67.6 24.2 %collective-permute-start.8 = (f32[552,256]{1,0:T(8,128)}, f32[552,256]{1,0:T(8,128)S(1)}, u32[]{:S(2)}, u32[]{:S(2)}) collective-permute-start(f32[552,256]{1,0:T(8,128)} %get-tuple-element.24), channel_id=1, source_target_pairs={{0,12},{4,16},{8,20},{12,24},{16,28},{20,0},{24,4},{28,8},{1,13},{... | collective-permute-start | bytes 1695752 | tf_op jit(solution)/shard_map/ppermute | solution.py:197
  67.6 85.4 %collective-permute-start.9 = (f32[552,256]{1,0:T(8,128)}, f32[552,256]{1,0:T(8,128)S(1)}, u32[]{:S(2)}, u32[]{:S(2)}) collective-permute-start(f32[552,256]{1,0:T(8,128)} %get-tuple-element.23), channel_id=1, source_target_pairs={{0,16},{4,20},{8,24},{12,28},{16,0},{20,4},{24,8},{28,12},{1,17},{... | collective-permute-start | bytes 1695752 | tf_op jit(solution)/shard_map/ppermute | solution.py:197
  70.7 83.2 %collective-permute-start.10 = (f32[552,256]{1,0:T(8,128)}, f32[552,256]{1,0:T(8,128)S(1)}, u32[]{:S(2)}, u32[]{:S(2)}) collective-permute-start(f32[552,256]{1,0:T(8,128)} %get-tuple-element.22), channel_id=1, source_target_pairs={{0,20},{4,24},{8,28},{12,0},{16,4},{20,8},{24,12},{28,16},{1,21},{... | collective-permute-start | bytes 1695752 | tf_op jit(solution)/shard_map/ppermute | solution.py:197
  70.7 84.1 %collective-permute-start.11 = (f32[552,256]{1,0:T(8,128)S(1)}, f32[552,256]{1,0:T(8,128)S(1)}, u32[]{:S(2)}, u32[]{:S(2)}) collective-permute-start(f32[552,256]{1,0:T(8,128)S(1)} %get-tuple-element.21), channel_id=1, source_target_pairs={{0,24},{4,28},{8,0},{12,4},{16,8},{20,12},{24,16},{28,20},{1,25},{... | collective-permute-start | bytes 1695752 | tf_op jit(solution)/shard_map/ppermute | solution.py:197
  79.7 75.9 %collective-permute-start.12 = (f32[552,256]{1,0:T(8,128)S(1)}, f32[552,256]{1,0:T(8,128)S(1)}, u32[]{:S(2)}, u32[]{:S(2)}) collective-permute-start(f32[552,256]{1,0:T(8,128)S(1)} %get-tuple-element.20), channel_id=1, source_target_pairs={{0,28},{4,0},{8,4},{12,8},{16,12},{20,16},{24,20},{28,24},{1,29},{... | collective-permute-start | bytes 1695752 | tf_op jit(solution)/shard_map/ppermute | solution.py:197
  157.4 17.3 %collective-permute-start.13 = (f32[32,256]{1,0:T(8,128)S(1)}, f32[32,256]{1,0:T(8,128)S(1)}, u32[]{:S(2)}, u32[]{:S(2)}) collective-permute-start(f32[32,256]{1,0:T(8,128)S(1)} %bitcast.95), channel_id=1, source_target_pairs={{0,4},{4,8},{8,12},{12,16},{16,20},{20,24},{24,28},{28,0},{1,5},{5... | collective-permute-start | bytes 98312 | tf_op jit(solution)/shard_map/ppermute | solution.py:208
  157.5 19.2 %collective-permute-start.14 = (f32[32,256]{1,0:T(8,128)S(1)}, f32[32,256]{1,0:T(8,128)S(1)}, u32[]{:S(2)}, u32[]{:S(2)}) collective-permute-start(f32[32,256]{1,0:T(8,128)S(1)} %bitcast.96), channel_id=1, source_target_pairs={{0,8},{4,12},{8,16},{12,20},{16,24},{20,28},{24,0},{28,4},{1,9},{5... | collective-permute-start | bytes 98312 | tf_op jit(solution)/shard_map/ppermute | solution.py:208
  158.4 19.0 %collective-permute-start.15 = (f32[32,256]{1,0:T(8,128)S(1)}, f32[32,256]{1,0:T(8,128)S(1)}, u32[]{:S(2)}, u32[]{:S(2)}) collective-permute-start(f32[32,256]{1,0:T(8,128)S(1)} %bitcast.97), channel_id=1, source_target_pairs={{0,12},{4,16},{8,20},{12,24},{16,28},{20,0},{24,4},{28,8},{1,13},{... | collective-permute-start | bytes 98312 | tf_op jit(solution)/shard_map/ppermute | solution.py:208
  164.9 12.6 %collective-permute-start.16 = (f32[32,256]{1,0:T(8,128)S(1)}, f32[32,256]{1,0:T(8,128)S(1)}, u32[]{:S(2)}, u32[]{:S(2)}) collective-permute-start(f32[32,256]{1,0:T(8,128)S(1)} %bitcast.98), channel_id=1, source_target_pairs={{0,16},{4,20},{8,24},{12,28},{16,0},{20,4},{24,8},{28,12},{1,17},{... | collective-permute-start | bytes 98312 | tf_op jit(solution)/shard_map/ppermute | solution.py:208
  164.9 12.6 %collective-permute-start.17 = (f32[32,256]{1,0:T(8,128)S(1)}, f32[32,256]{1,0:T(8,128)S(1)}, u32[]{:S(2)}, u32[]{:S(2)}) collective-permute-start(f32[32,256]{1,0:T(8,128)S(1)} %bitcast.99), channel_id=1, source_target_pairs={{0,20},{4,24},{8,28},{12,0},{16,4},{20,8},{24,12},{28,16},{1,21},{... | collective-permute-start | bytes 98312 | tf_op jit(solution)/shard_map/ppermute | solution.py:208
  174.7 4.6 %collective-permute-start.18 = (f32[32,256]{1,0:T(8,128)S(1)}, f32[32,256]{1,0:T(8,128)S(1)}, u32[]{:S(2)}, u32[]{:S(2)}) collective-permute-start(f32[32,256]{1,0:T(8,128)S(1)} %bitcast.100), channel_id=1, source_target_pairs={{0,24},{4,28},{8,0},{12,4},{16,8},{20,12},{24,16},{28,20},{1,25},{... | collective-permute-start | bytes 98312 | tf_op jit(solution)/shard_map/ppermute | solution.py:208
  176.7 5.1 %collective-permute-start.19 = (f32[32,256]{1,0:T(8,128)S(1)}, f32[32,256]{1,0:T(8,128)S(1)}, u32[]{:S(2)}, u32[]{:S(2)}) collective-permute-start(f32[32,256]{1,0:T(8,128)S(1)} %bitcast.101), channel_id=1, source_target_pairs={{0,28},{4,0},{8,4},{12,8},{16,12},{20,16},{24,20},{28,24},{1,29},{... | collective-permute-start | bytes 98312 | tf_op jit(solution)/shard_map/ppermute | solution.py:208
  182.0 0.7 copy-start.1

commit v2 on v1

--- a/solution.py
+++ b/solution.py
@@ -82,21 +82,22 @@
     )(rows, slots, count, tile_values, partition, extra)
 
 
-def _combine_kernel(map_ref, recv_ref, out_ref):
+def _combine_kernel(map_ref, recv_ref, init_ref, out_ref):
     g = pl.program_id(0)
     tile_size = out_ref.shape[1]
 
     @pl.when(g == 0)
     def _():
-        out_ref[...] = jnp.zeros(out_ref.shape, out_ref.dtype)
+        out_ref[...] = init_ref[...]
 
     for k in range(CAP):
         b = map_ref[g * CAP + k]
         out_ref[b] += recv_ref[0, k * tile_size:(k + 1) * tile_size, :]
 
 
-def _combine(block_map, received, out_blocks, tile_size):
+def _combine(block_map, received, init):
     total, _, width = received.shape
+    out_blocks, tile_size, _ = init.shape
 
     def recv_map(g, map_ref):
         return (g, 0, 0)
@@ -110,16 +111,19 @@
         grid_spec=pltpu.PrefetchScalarGridSpec(
             num_scalar_prefetch=1,
             grid=(total,),
-            in_specs=[pl.BlockSpec((1, CAP * tile_size, width), recv_map)],
+            in_specs=[
+                pl.BlockSpec((1, CAP * tile_size, width), recv_map),
+                pl.BlockSpec((out_blocks, tile_size, width), whole),
+            ],
             out_specs=pl.BlockSpec((out_blocks, tile_size, width), whole),
         ),
         compiler_params=pltpu.CompilerParams(dimension_semantics=("arbitrary",)),
         cost_estimate=pl.CostEstimate(
             flops=total * CAP * tile_size * width,
             transcendentals=0,
-            bytes_accessed=(total * CAP + out_blocks) * tile_size * width * 4,
-        ),
-    )(block_map, received)
+            bytes_accessed=(total * CAP + 2 * out_blocks) * tile_size * width * 4,
+        ),
+    )(block_map, received, init)
 
 
 def _pick(stacked, index):
@@ -176,32 +180,62 @@
         [jnp.sum(jnp.where((rank == k) & (present > 0), block_ids[None, :], 0), axis=1) for k in range(CAP)],
         axis=1,
     )
+    half = dom_count // 2
+    side = dom_index // half
+    pos = dom_index % half
+    dest_dom = cols // local_blocks
+    cross = (dest_dom // half != side).astype(jnp.int32)
+    slots = (cross * half + (dest_dom % half - pos) % half) * CAP + tile_rank
+    order = jnp.arange(dom_count, dtype=jnp.int32)
+    order_side = jnp.where(order // half == 0, side, 1 - side)
+    order = order_side * half + (pos + order % half) % half
     dom_ids = jnp.arange(dom_count, dtype=jnp.int32)
-    rotate = ((dom_ids[:, None] + dom_index) % dom_count) == dom_ids[None, :]
+    rotate = order[:, None] == dom_ids[None, :]
     table = jnp.sum(jnp.where(rotate[:, :, None], table[None, :, :], 0), axis=1)
-    dest_dom = cols // local_blocks
-    slots = ((dest_dom - dom_index) % dom_count) * CAP + tile_rank
 
     chunk = width // dom_count
     chunks = loop_sum.reshape(dom_count, chunk, width)
-    chunks = jnp.stack([_pick(chunks, (dom_index + shift) % dom_count) for shift in range(dom_count)])
+    chunks = jnp.stack([_pick(chunks, order[i]) for i in range(dom_count)])
     id_rows = jnp.zeros((dom_count, 8, width), jnp.float32)
     id_rows = id_rows.at[:, 0, :CAP].set(table.astype(jnp.float32))
     extra = jnp.concatenate([chunks, id_rows], axis=1)
 
     compact = _spmm(rows, slots, tile_counts, tile_values, partition, extra)
-
+    body_rows = CAP * tile_size
+
+    def within(shift):
+        return [(i, (i // half) * half + (i % half + shift) % half) for i in range(dom_count)]
+
+    swap = [(i, (1 - i // half) * half + i % half) for i in range(dom_count)]
+
+    def unpack(slabs):
+        ids = slabs[:, body_rows + chunk, :CAP].astype(jnp.int32).reshape(-1)
+        total = slabs[0, body_rows:body_rows + chunk, :]
+        for k in range(1, slabs.shape[0]):
+            total = total + slabs[k, body_rows:body_rows + chunk, :]
+        return ids, total
+
+    relay = [compact[half]]
+    for shift in range(1, half):
+        relay.append(lax.ppermute(compact[half + shift], "dom", within(shift)))
+    relay = jnp.stack(relay)
+    relay_ids, relay_chunk = unpack(relay)
+    zeros = jnp.zeros((local_blocks, tile_size, width), jnp.float32)
+    dense = _combine(relay_ids, relay, zeros)
+    payload = jnp.concatenate([dense.reshape(node_rows, width), relay_chunk], axis=0)
+
+    direct = [compact[shift] for shift in range(1, half)]
+    direct, payload = lax.optimization_barrier((direct, payload))
+    partner = lax.ppermute(payload, "dom", swap)
     received = [compact[0]]
-    for shift in range(1, dom_count):
-        pairs = [(i, (i + shift) % dom_count) for i in range(dom_count)]
-        received.append(lax.ppermute(compact[shift], "dom", pairs))
+    for shift in range(1, half):
+        received.append(lax.ppermute(direct[shift - 1], "dom", within(shift)))
     received = jnp.stack(received)
-    body_rows = CAP * tile_size
-    parts = received[:, body_rows:body_rows + chunk, :]
-    block_map = received[:, body_rows + chunk, :CAP].astype(jnp.int32).reshape(-1)
-    own = _pick(parts, dom_index % dom_count)
-    for source in range(1, dom_count):
-        own = own + _pick(parts, (dom_index - source) % dom_count)
+    ids, own = unpack(received)
+    own = own + partner[node_rows:]
+    node_grad = _combine(ids, received, partner[:node_rows].reshape(local_blocks, tile_size, width))
+    node_grad = node_grad.reshape(node_rows, width)
+
     gathered = [own]
     for shift in range(1, dom_count):
         pairs = [(i, (i + shift) % dom_count) for i in range(dom_count)]
@@ -210,7 +244,6 @@
     weight_grad = jnp.concatenate(
         [_pick(gathered, (dom_index - k) % dom_count) for k in range(dom_count)], axis=0
     )
-    node_grad = _combine(block_map, received, local_blocks, tile_size).reshape(node_rows, width)
     return (node_grad, weight_grad)
 
 

time: 186 us -> 178 us (0.957)
  the two profiles are of different devices: /device:TPU:31 before, /device:TPU:7 now
where the time goes in v2:
time: 178 us; the launch traced here: 177 us
  waiting for transfers between devices  62.2 us (35%)
  starting transfers between devices  43.4 us (24%)
  Pallas kernels  33.8 us (19%)
  between operations  16.6 us (9%)
  local copies, waits for them, and re-layouts  11 us (6%)
  other arithmetic  6.96 us (4%)
  matrix products  3.15 us (2%)
    ppermute x3, waiting for transfers between devices, shards(): received.append(lax.ppermute(direct[shift - 1], 'dom', within(shift)))  29.1 us
    ppermute x7, starting transfers between devices, shards(): gathered.append(lax.ppermute(own, 'dom', pairs))  25.8 us
    pallas_call x1, Pallas kernels, _spmm(): pl.pallas_call(_spmm_kernel, out_shape=jax.ShapeDtypeStruct((dests, out_r...  24.9 us
    ppermute x3, waiting for transfers between devices, shards(): relay.append(lax.ppermute(compact[half + shift], 'dom', within(shift)))  16.9 us
    ppermute x6, waiting for transfers between devices, shards(): piece, term = lax.ppermute((projected, weight_term), 'loop', pairs)  11.5 us
    ppermute x3, starting transfers between devices, shards(): received.append(lax.ppermute(direct[shift - 1], 'dom', within(shift)))  10.3 us
    pallas_call x2, Pallas kernels, _combine(): pl.pallas_call(_combine_kernel, out_shape=jax.ShapeDtypeStruct((out_block...  8.87 us
    ppermute x6, starting transfers between devices, shards(): piece, term = lax.ppermute((projected, weight_term), 'loop', pairs)  5.45 us
  transfers between devices with their start and end apart: 20, of which 9 were waited for; matrix products, arithmetic and copies ran while one was open for 5% of the time, Pallas kernels for 3%

profile of v2, /device:TPU:7, one launch (start us, length us, event | category | flops | bytes accessed | tf_op | source)
XLA Modules:
  0.0 177.1 jit_solution(14446446506538567889)
XLA Ops:
  0.7 1.6 convolution_convert_fusion
  2.6 1.5 convolution_multiply_fusion
  4.2 2.4 %collective-permute-start.5 = (f32[256,256]{1,0:T(8,128)S(1)}, f32[256,256]{1,0:T(8,128)S(1)}, u32[]{:S(2)}, u32[]{:S(2)}) collective-permute-start(f32[256,256]{1,0:T(8,128)S(1)} %bitcast.110), channel_id=1, source_target_pairs={{0,3},{1,0},{2,1},{3,2},{4,7},{5,4},{6,5},{7,6},{8,11},{9,8},{10,9... | collective-permute-start | bytes 786440 | tf_op jit(solution)/shard_map/ppermute | solution.py:154
  26.7 11.5 %collective-permute-done.4 = f32[256,256]{1,0:T(8,128)S(1)} collective-permute-done((f32[256,256]{1,0:T(8,128)S(1)}, f32[256,256]{1,0:T(8,128)S(1)}, u32[]{:S(2)}, u32[]{:S(2)}) %collective-permute-start.4) | collective-permute-done | bytes 262176 | tf_op jit(solution)/shard_map/ppermute | solution.py:154
  38.7 24.9 %shard_map.95 = f32[8,552,256]{2,1,0:T(8,128)} custom-call(s32[640]{0:T(1024)S(1)} %get-tuple-element.45.rows_ref, s32[640]{0:T(1024)S(1)} %get-tuple-element.46.slots_ref, s32[1]{0:T(128)} %copy.34.cnt_ref, bf16[640,128,128]{2,1,0:T(8,128)(2,1)} %tv_ref.1, bf16[32,128,256]{2,1,0:T(8,128)(2,1)S(1)} %bitcast.86, f32[8,40,256]{2,1,0:T(8,128)S(1)} %select_maximum_fusion.extra_ref), custom_call_target="tpu_custom_call" | custom-call | flops 5368709120 | bytes 25493504 | tf_op jit(solution)/shard_map/pallas_call | solution.py:60
  63.6 3.7 %fusion.27 = (f32[1,552,256]{2,1,0:T(8,128)S(1)}, f32[552,256]{1,0:T(8,128)S(1)}, f32[552,256]{1,0:T(8,128)S(1)}, f32[552,256]{1,0:T(8,128)S(1)}, f32[1,552,256]...) fusion(f32[8,552,256]{2,1,0:T(8,128)} %shard_map.95), kind=kLoop, calls=%fused_computation.122 | loop fusion | bytes 9043968 | tf_op jit(solution)/shard_map/slice | solution.py:230
  67.3 1.8 collective-permute-start.6
  69.1 13.5 %collective-permute-done.8 = f32[552,256]{1,0:T(8,128)S(1)} collective-permute-done((f32[552,256]{1,0:T(8,128)S(1)}, f32[552,256]{1,0:T(8,128)S(1)}, u32[]{:S(2)}, u32[]{:S(2)}) %collective-permute-start.8) | collective-permute-done | bytes 565280 | tf_op jit(solution)/shard_map/ppermute | solution.py:220
  82.6 3.4 %collective-permute-done.6 = f32[552,256]{1,0:T(8,128)S(1)} collective-permute-done((f32[552,256]{1,0:T(8,128)S(1)}, f32[552,256]{1,0:T(8,128)S(1)}, u32[]{:S(2)}, u32[]{:S(2)}) %collective-permute-start.6) | collective-permute-done | bytes 565280 | tf_op jit(solution)/shard_map/ppermute | solution.py:220
  88.7 4.4 %shard_map.96 = f32[8,128,256]{2,1,0:T(8,128)} custom-call(s32[16]{0:T(128)} %convert_element_type.41.map_ref, f32[4,552,256]{2,1,0:T(8,128)} %copy-done.2, f32[8,128,256]{2,1,0:T(8,128)} %broadcast_in_dim.81.init_ref), custom_call_target="tpu_custom_call" | custom-call | flops 524288 | bytes 4194304 | tf_op jit(solution)/shard_map/pallas_call | solution.py:108
  93.1 2.4 %pad_maximum_fusion.3 = f32[1056,256]{1,0:T(8,128)} fusion(f32[32,256]{1,0:T(8,128)S(1)} %fusion.3, f32[1024,256]{1,0:T(8,128)} %bitcast.87), kind=kLoop, calls=%fused_computation.5 | loop fusion | flops 270336 | bytes 2162688 | tf_op jit(solution)/shard_map/concatenate | solution.py:225
  95.5 8.7 %collective-permute-start.11 = (f32[552,256]{1,0:T(8,128)}, f32[552,256]{1,0:T(8,128)S(1)}, u32[]{:S(2)}, u32[]{:S(2)}) collective-permute-start(f32[552,256]{1,0:T(8,128)} %get-tuple-element.20), channel_id=1, source_target_pairs={{0,12},{4,0},{8,4},{12,8},{16,28},{20,16},{24,20},{28,24},{1,13},{... | collective-permute-start | bytes 1695752 | tf_op jit(solution)/shard_map/ppermute | solution.py:232
  104.2 1.6 collective-permute-start.9
  105.8 11.2 %collective-permute-done.11 = f32[552,256]{1,0:T(8,128)S(1)} collective-permute-done((f32[552,256]{1,0:T(8,128)}, f32[552,256]{1,0:T(8,128)S(1)}, u32[]{:S(2)}, u32[]{:S(2)}) %collective-permute-start.11) | collective-permute-done | bytes 565280 | tf_op jit(solution)/shard_map/ppermute | solution.py:232
  117.1 5.7 %collective-permute-done.10 = f32[552,256]{1,0:T(8,128)S(1)} collective-permute-done((f32[552,256]{1,0:T(8,128)}, f32[552,256]{1,0:T(8,128)S(1)}, u32[]{:S(2)}, u32[]{:S(2)}) %collective-permute-start.10) | collective-permute-done | bytes 565280 | tf_op jit(solution)/shard_map/ppermute | solution.py:232
  122.8 12.1 %collective-permute-done.9 = f32[552,256]{1,0:T(8,128)S(1)} collective-permute-done((f32[552,256]{1,0:T(8,128)}, f32[552,256]{1,0:T(8,128)S(1)}, u32[]{:S(2)}, u32[]{:S(2)}) %collective-permute-start.9) | collective-permute-done | bytes 565280 | tf_op jit(solution)/shard_map/ppermute | solution.py:232
  135.8 1.6 pad_maximum_fusion.1.recv_ref
  139.7 10.2 %collective-permute-start.13 = (f32[32,256]{1,0:T(8,128)S(1)}, f32[32,256]{1,0:T(8,128)S(1)}, u32[]{:S(2)}, u32[]{:S(2)}) collective-permute-start(f32[32,256]{1,0:T(8,128)S(1)} %get-tuple-element.27), channel_id=1, source_target_pairs={{0,4},{4,8},{8,12},{12,16},{16,20},{20,24},{24,28},{28,0},{1,5},{5... | collective-permute-start | bytes 98312 | tf_op jit(solution)/shard_map/ppermute | solution.py:242
  150.6 9.4 %collective-permute-start.14 = (f32[32,256]{1,0:T(8,128)S(1)}, f32[32,256]{1,0:T(8,128)S(1)}, u32[]{:S(2)}, u32[]{:S(2)}) collective-permute-start(f32[32,256]{1,0:T(8,128)S(1)} %get-tuple-element.27), channel_id=1, source_target_pairs={{0,8},{4,12},{8,16},{12,20},{16,24},{20,28},{24,0},{28,4},{1,9},{5... | collective-permute-start | bytes 98312 | tf_op jit(solution)/shard_map/ppermute | solution.py:242
  159.9 2.1 %collective-permute-start.15 = (f32[32,256]{1,0:T(8,128)S(1)}, f32[32,256]{1,0:T(8,128)S(1)}, u32[]{:S(2)}, u32[]{:S(2)}) collective-permute-start(f32[32,256]{1,0:T(8,128)S(1)} %get-tuple-element.27), channel_id=1, source_target_pairs={{0,12},{4,16},{8,20},{12,24},{16,28},{20,0},{24,4},{28,8},{1,13},{... | collective-permute-start | bytes 98312 | tf_op jit(solution)/shard_map/ppermute | solution.py:242
  162.1 2.7 %collective-permute-start.17 = (f32[32,256]{1,0:T(8,128)S(1)}, f32[32,256]{1,0:T(8,128)S(1)}, u32[]{:S(2)}, u32[]{:S(2)}) collective-permute-start(f32[32,256]{1,0:T(8,128)S(1)} %get-tuple-element.27), channel_id=1, source_target_pairs={{0,20},{4,24},{8,28},{12,0},{16,4},{20,8},{24,12},{28,16},{1,21},{... | collective-permute-start | bytes 98312 | tf_op jit(solution)/shard_map/ppermute | solution.py:242
  164.7 2.3 %slice.151 = f32[1024,256]{1,0:T(8,128)} slice(f32[1056,256]{1,0:T(8,128)} %collective-permute-done.12), slice={[0:1024], [0:256]} | slice | bytes 2097152 | tf_op jit(solution)/shard_map/slice | solution.py:236
  167.0 4.4 %shard_map.97 = f32[8,128,256]{2,1,0:T(8,128)} custom-call(s32[16]{0:T(128)} %convert_element_type.43.map_ref, f32[4,552,256]{2,1,0:T(8,128)} %copy-done.1, f32[8,128,256]{2,1,0:T(8,128)} %bitcast.88), custom_call_target="tpu_custom_call" | custom-call | flops 524288 | bytes 4194304 | tf_op jit(solution)/shard_map/pallas_call | solution.py:108
  174.2 2.0 %collective-permute-done.19 = f32[32,256]{1,0:T(8,128)S(1)} collective-permute-done((f32[32,256]{1,0:T(8,128)S(1)}, f32[32,256]{1,0:T(8,128)S(1)}, u32[]{:S(2)}, u32[]{:S(2)}) %collective-permute-start.19) | collective-permute-done | bytes 32800 | tf_op jit(solution)/shard_map/ppermute | solution.py:242
  (96 shorter events, 15.3 us)
Async XLA Ops:
  0.7 19.6 %copy-start.8 = (s32[1,640]{1,0:T(1,128)S(1)}, s32[1,640]{1,0:T(1,128)}, u32[]{:S(2)}) copy-start(s32[1,640]{1,0:T(1,128)} %param.15) | copy-start | bytes 7684
  2.3 36.3 %collective-permute-start.2 = (bf16[1024,256]{1,0:T(8,128)(2,1)S(1)}, bf16[1024,256]{1,0:T(8,128)(2,1)S(1)}, u32[]{:S(2)}, u32[]{:S(2)}) collective-permute-start(bf16[1024,256]{1,0:T(8,128)(2,1)S(1)} %convolution_convert_fusion), channel_id=1, source_target_pairs={{0,3},{1,0},{2,1},{3,2},{4,7},{5,4},{6,5},{7,6},{8,11},{9,8},{10,9... | collective-permute-start | bytes 1572872 | tf_op jit(solution)/shard_map/ppermute | solution.py:154
  2.6 36.0 %collective-permute-start.1 = (bf16[1024,256]{1,0:T(8,128)(2,1)S(1)}, bf16[1024,256]{1,0:T(8,128)(2,1)S(1)}, u32[]{:S(2)}, u32[]{:S(2)}) collective-permute-start(bf16[1024,256]{1,0:T(8,128)(2,1)S(1)} %convolution_convert_fusion), channel_id=1, source_target_pairs={{0,2},{1,3},{2,0},{3,1},{4,6},{5,7},{6,4},{7,5},{8,10},{9,11},{10,... | collective-permute-start | bytes 1572872 | tf_op jit(solution)/shard_map/ppermute | solution.py:154
  4.2 21.2 %collective-permute-start.5 = (f32[256,256]{1,0:T(8,128)S(1)}, f32[256,256]{1,0:T(8,128)S(1)}, u32[]{:S(2)}, u32[]{:S(2)}) collective-permute-start(f32[256,256]{1,0:T(8,128)S(1)} %bitcast.110), channel_id=1, source_target_pairs={{0,3},{1,0},{2,1},{3,2},{4,7},{5,4},{6,5},{7,6},{8,11},{9,8},{10,9... | collective-permute-start | bytes 786440 | tf_op jit(solution)/shard_map/ppermute | solution.py:154
  6.6 31.6 %collective-permute-start.4 = (f32[256,256]{1,0:T(8,128)S(1)}, f32[256,256]{1,0:T(8,128)S(1)}, u32[]{:S(2)}, u32[]{:S(2)}) collective-permute-start(f32[256,256]{1,0:T(8,128)S(1)} %bitcast.111), channel_id=1, source_target_pairs={{0,2},{1,3},{2,0},{3,1},{4,6},{5,7},{6,4},{7,5},{8,10},{9,11},{10,... | collective-permute-start | bytes 786440 | tf_op jit(solution)/shard_map/ppermute | solution.py:154
  6.8 31.4 %collective-permute-start.3 = (f32[256,256]{1,0:T(8,128)S(1)}, f32[256,256]{1,0:T(8,128)S(1)}, u32[]{:S(2)}, u32[]{:S(2)}) collective-permute-start(f32[256,256]{1,0:T(8,128)S(1)} %bitcast.112), channel_id=1, source_target_pairs={{0,1},{1,2},{2,3},{3,0},{4,5},{5,6},{6,7},{7,4},{8,9},{9,10},{10,1... | collective-permute-start | bytes 786440 | tf_op jit(solution)/shard_map/ppermute | solution.py:154
  25.4 13.2 %collective-permute-start = (bf16[1024,256]{1,0:T(8,128)(2,1)S(1)}, bf16[1024,256]{1,0:T(8,128)(2,1)S(1)}, u32[]{:S(2)}, u32[]{:S(2)}) collective-permute-start(bf16[1024,256]{1,0:T(8,128)(2,1)S(1)} %convolution_convert_fusion), channel_id=1, source_target_pairs={{0,1},{1,2},{2,3},{3,0},{4,5},{5,6},{6,7},{7,4},{8,9},{9,10},{10,1... | collective-permute-start | bytes 1572872 | tf_op jit(solution)/shard_map/ppermute | solution.py:154
  67.3 15.3 %collective-permute-start.8 = (f32[552,256]{1,0:T(8,128)S(1)}, f32[552,256]{1,0:T(8,128)S(1)}, u32[]{:S(2)}, u32[]{:S(2)}) collective-permute-start(f32[552,256]{1,0:T(8,128)S(1)} %get-tuple-element.29), channel_id=1, source_target_pairs={{0,12},{4,0},{8,4},{12,8},{16,28},{20,16},{24,20},{28,24},{1,13},{... | collective-permute-start | bytes 1695752 | tf_op jit(solution)/shard_map/ppermute | solution.py:220
  67.3 15.3 %collective-permute-start.7 = (f32[552,256]{1,0:T(8,128)S(1)}, f32[552,256]{1,0:T(8,128)S(1)}, u32[]{:S(2)}, u32[]{:S(2)}) collective-permute-start(f32[552,256]{1,0:T(8,128)S(1)} %get-tuple-element.30), channel_id=1, source_target_pairs={{0,8},{4,12},{8,0},{12,4},{16,24},{20,28},{24,16},{28,20},{1,9},{5... | collective-permute-start | bytes 1695752 | tf_op jit(solution)/shard_map/ppermute | solution.py:220
  67.3 18.7 %collective-permute-start.6 = (f32[552,256]{1,0:T(8,128)S(1)}, f32[552,256]{1,0:T(8,128)S(1)}, u32[]{:S(2)}, u32[]{:S(2)}) collective-permute-start(f32[552,256]{1,0:T(8,128)S(1)} %get-tuple-element.31), channel_id=1, source_target_pairs={{0,4},{4,8},{8,12},{12,0},{16,20},{20,24},{24,28},{28,16},{1,5},{5... | collective-permute-start | bytes 1695752 | tf_op jit(solution)/shard_map/ppermute | solution.py:220
  95.5 43.4 %collective-permute-start.12 = (f32[1056,256]{1,0:T(8,128)}, f32[1056,256]{1,0:T(8,128)}, u32[]{:S(2)}, u32[]{:S(2)}) collective-permute-start(f32[1056,256]{1,0:T(8,128)} %pad_maximum_fusion.3), channel_id=1, source_target_pairs={{0,16},{4,20},{8,24},{12,28},{16,0},{20,4},{24,8},{28,12},{1,17},{... | collective-permute-start | bytes 3244040 | tf_op jit(solution)/shard_map/ppermute | solution.py:229
  95.5 21.6 %collective-permute-start.11 = (f32[552,256]{1,0:T(8,128)}, f32[552,256]{1,0:T(8,128)S(1)}, u32[]{:S(2)}, u32[]{:S(2)}) collective-permute-start(f32[552,256]{1,0:T(8,128)} %get-tuple-element.20), channel_id=1, source_target_pairs={{0,12},{4,0},{8,4},{12,8},{16,28},{20,16},{24,20},{28,24},{1,13},{... | collective-permute-start | bytes 1695752 | tf_op jit(solution)/shard_map/ppermute | solution.py:232
  104.2 18.6 %collective-permute-start.10 = (f32[552,256]{1,0:T(8,128)}, f32[552,256]{1,0:T(8,128)S(1)}, u32[]{:S(2)}, u32[]{:S(2)}) collective-permute-start(f32[552,256]{1,0:T(8,128)} %get-tuple-element.19), channel_id=1, source_target_pairs={{0,8},{4,12},{8,0},{12,4},{16,24},{20,28},{24,16},{28,20},{1,9},{5... | collective-permute-start | bytes 1695752 | tf_op jit(solution)/shard_map/ppermute | solution.py:232
  104.2 30.7 %collective-permute-start.9 = (f32[552,256]{1,0:T(8,128)}, f32[552,256]{1,0:T(8,128)S(1)}, u32[]{:S(2)}, u32[]{:S(2)}) collective-permute-start(f32[552,256]{1,0:T(8,128)} %get-tuple-element.18), channel_id=1, source_target_pairs={{0,4},{4,8},{8,12},{12,0},{16,20},{20,24},{24,28},{28,16},{1,5},{5... | collective-permute-start | bytes 1695752 | tf_op jit(solution)/shard_map/ppermute | solution.py:232
  117.1 17.8 %copy-start.3 = (f32[552,256]{1,0:T(8,128)}, f32[552,256]{1,0:T(8,128)S(1)}, u32[]{:S(2)}) copy-start(f32[552,256]{1,0:T(8,128)S(1)} %collective-permute-done.11) | copy-start | bytes 1695748
  122.8 12.1 %copy-start.4 = (f32[552,256]{1,0:T(8,128)}, f32[552,256]{1,0:T(8,128)S(1)}, u32[]{:S(2)}) copy-start(f32[552,256]{1,0:T(8,128)S(1)} %collective-permute-done.10) | copy-start | bytes 1695748
  137.4 29.6 %copy-start.1 = (f32[4,552,256]{2,1,0:T(8,128)}, f32[4,552,256]{2,1,0:T(8,128)S(1)}, u32[]{:S(2)}) copy-start(f32[4,552,256]{2,1,0:T(8,128)S(1)} %pad_maximum_fusion.1.recv_ref) | copy-start | bytes 6782980
  139.7 31.7 %collective-permute-start.13 = (f32[32,256]{1,0:T(8,128)S(1)}, f32[32,256]{1,0:T(8,128)S(1)}, u32[]{:S(2)}, u32[]{:S(2)}) collective-permute-start(f32[32,256]{1,0:T(8,128)S(1)} %get-tuple-element.27), channel_id=1, source_target_pairs={{0,4},{4,8},{8,12},{12,16},{16,20},{20,24},{24,28},{28,0},{1,5},{5... | collective-permute-start | bytes 98312 | tf_op jit(solution)/shard_map/ppermute | solution.py:242
  150.6 22.3 %collective-permute-start.14 = (f32[32,256]{1,0:T(8,128)S(1)}, f32[32,256]{1,0:T(8,128)S(1)}, u32[]{:S(2)}, u32[]{:S(2)}) collective-permute-start(f32[32,256]{1,0:T(8,128)S(1)} %get-tuple-element.27), channel_id=1, source_target_pairs={{0,8},{4,12},{8,16},{12,20},{16,24},{20,28},{24,0},{28,4},{1,9},{5... | collective-permute-start | bytes 98312 | tf_op jit(solution)/shard_map/ppermute | solution.py:242
  159.9 13.0 %collective-permute-start.15 = (f32[32,256]{1,0:T(8,128)S(1)}, f32[32,256]{1,0:T(8,128)S(1)}, u32[]{:S(2)}, u32[]{:S(2)}) collective-permute-start(f32[32,256]{1,0:T(8,128)S(1)} %get-tuple-element.27), channel_id=1, source_target_pairs={{0,12},{4,16},{8,20},{12,24},{16,28},{20,0},{24,4},{28,8},{1,13},{... | collective-permute-start | bytes 98312 | tf_op jit(solution)/shard_map/ppermute | solution.py:242
  162.0 10.9 %collective-permute-start.16 = (f32[32,256]{1,0:T(8,128)S(1)}, f32[32,256]{1,0:T(8,128)S(1)}, u32[]{:S(2)}, u32[]{:S(2)}) collective-permute-start(f32[32,256]{1,0:T(8,128)S(1)} %get-tuple-element.27), channel_id=1, source_target_pairs={{0,16},{4,20},{8,24},{12,28},{16,0},{20,4},{24,8},{28,12},{1,17},{... | collective-permute-start | bytes 98312 | tf_op jit(solution)/shard_map/ppermute | solution.py:242
  162.1 10.9 %collective-permute-start.17 = (f32[32,256]{1,0:T(8,128)S(1)}, f32[32,256]{1,0:T(8,128)S(1)}, u32[]{:S(2)}, u32[]{:S(2)}) collective-permute-start(f32[32,256]{1,0:T(8,128)S(1)} %get-tuple-element.27), channel_id=1, source_target_pairs={{0,20},{4,24},{8,28},{12,0},{16,4},{20,8},{24,12},{28,16},{1,21},{... | collective-permute-start | bytes 98312 | tf_op jit(solution)/shard_map/ppermute | solution.py:242
  171.4 2.8 %collective-permute-start.18 = (f32[32,256]{1,0:T(8,128)S(1)}, f32[32,256]{1,0:T(8,128)S(1)}, u32[]{:S(2)}, u32[]{:S(2)}) collective-permute-start(f32[32,256]{1,0:T(8,128)S(1)} %get-tuple-element.27), channel_id=1, source_target_pairs={{0,24},{4,28},{8,0},{12,4},{16,8},{20,12},{24,16},{28,20},{1,25},{... | collective-permute-start | bytes 98312 | tf_op jit(solution)/shard_map/ppermute | solution.py:242
  172.9 3.3 %collective-permute-start.19 = (f32[32,256]{1,0:T(8,128)S(1)}, f32[32,256]{1,0:T(8,128)S(1)}, u32[]{:S(2)}, u32[]{:S(2)}) collective-permute-start(f32[32,256]{1,0:T(8,128)S(1)} %get-tuple-element.27), channel_id=1, source_target_pairs={{0,28},{4,0},{8,4},{12,8},{16,12},{20,16},{24,20},{28,24},{1,29},{... | collective-permute-start | bytes 98312 | tf_op jit(solution)/shard_map/ppermute | solution.py:242
  (5 other events, 12.7 us)

commit v3 on v2

--- a/solution.py
+++ b/solution.py
@@ -148,15 +148,17 @@
     projected = jnp.dot(masked, weight.T, preferred_element_type=jnp.float32).astype(jnp.bfloat16)
 
     pieces = [projected]
+    for shift in range(1, loop_count):
+        pairs = [(i, (i + shift) % loop_count) for i in range(loop_count)]
+        pieces.append(lax.ppermute(projected, "loop", pairs))
+    partition = jnp.concatenate(pieces, axis=0).reshape(
+        loop_count * local_blocks, tile_size, width
+    )
+    partition, weight_term = lax.optimization_barrier((partition, weight_term))
     terms = [weight_term]
     for shift in range(1, loop_count):
         pairs = [(i, (i + shift) % loop_count) for i in range(loop_count)]
-        piece, term = lax.ppermute((projected, weight_term), "loop", pairs)
-        pieces.append(piece)
-        terms.append(term)
-    partition = jnp.concatenate(pieces, axis=0).reshape(
-        loop_count * local_blocks, tile_size, width
-    )
+        terms.append(lax.ppermute(weight_term, "loop", pairs))
     terms = jnp.stack(terms)
     loop_sum = _pick(terms, loop_index % loop_count)
     for source in range(1, loop_count):
@@ -194,14 +196,20 @@
     table = jnp.sum(jnp.where(rotate[:, :, None], table[None, :, :], 0), axis=1)
 
     chunk = width // dom_count
-    chunks = loop_sum.reshape(dom_count, chunk, width)
-    chunks = jnp.stack([_pick(chunks, order[i]) for i in range(dom_count)])
     id_rows = jnp.zeros((dom_count, 8, width), jnp.float32)
     id_rows = id_rows.at[:, 0, :CAP].set(table.astype(jnp.float32))
-    extra = jnp.concatenate([chunks, id_rows], axis=1)
+    extra = jnp.concatenate([jnp.zeros((dom_count, 2 * chunk, width), jnp.float32), id_rows], axis=1)
 
     compact = _spmm(rows, slots, tile_counts, tile_values, partition, extra)
     body_rows = CAP * tile_size
+    chunks = loop_sum.reshape(dom_count, chunk, width)
+    first = jnp.stack([_pick(chunks, order[i]) for i in range(dom_count)])
+    second = jnp.concatenate(
+        [jnp.zeros((half, chunk, width), jnp.float32), first[:half]], axis=0
+    )
+    compact = lax.dynamic_update_slice(
+        compact, jnp.concatenate([first, second], axis=1), (0, body_rows, 0)
+    )
 
     def within(shift):
         return [(i, (i // half) * half + (i % half + shift) % half) for i in range(dom_count)]
@@ -209,20 +217,22 @@
     swap = [(i, (1 - i // half) * half + i % half) for i in range(dom_count)]
 
     def unpack(slabs):
-        ids = slabs[:, body_rows + chunk, :CAP].astype(jnp.int32).reshape(-1)
-        total = slabs[0, body_rows:body_rows + chunk, :]
+        ids = slabs[:, body_rows + 2 * chunk, :CAP].astype(jnp.int32).reshape(-1)
+        relayed = slabs[0, body_rows:body_rows + chunk, :]
+        kept = slabs[0, body_rows + chunk:body_rows + 2 * chunk, :]
         for k in range(1, slabs.shape[0]):
-            total = total + slabs[k, body_rows:body_rows + chunk, :]
-        return ids, total
+            relayed = relayed + slabs[k, body_rows:body_rows + chunk, :]
+            kept = kept + slabs[k, body_rows + chunk:body_rows + 2 * chunk, :]
+        return ids, relayed, kept
 
     relay = [compact[half]]
     for shift in range(1, half):
         relay.append(lax.ppermute(compact[half + shift], "dom", within(shift)))
     relay = jnp.stack(relay)
-    relay_ids, relay_chunk = unpack(relay)
+    relay_ids, relay_chunk, own = unpack(relay)
+    own = own + lax.ppermute(relay_chunk, "dom", swap)
     zeros = jnp.zeros((local_blocks, tile_size, width), jnp.float32)
-    dense = _combine(relay_ids, relay, zeros)
-    payload = jnp.concatenate([dense.reshape(node_rows, width), relay_chunk], axis=0)
+    payload = _combine(relay_ids, relay, zeros)
 
     direct = [compact[shift] for shift in range(1, half)]
     direct, payload = lax.optimization_barrier((direct, payload))
@@ -231,10 +241,8 @@
     for shift in range(1, half):
         received.append(lax.ppermute(direct[shift - 1], "dom", within(shift)))
     received = jnp.stack(received)
-    ids, own = unpack(received)
-    own = own + partner[node_rows:]
-    node_grad = _combine(ids, received, partner[:node_rows].reshape(local_blocks, tile_size, width))
-    node_grad = node_grad.reshape(node_rows, width)
+    ids = received[:, body_rows + 2 * chunk, :CAP].astype(jnp.int32).reshape(-1)
+    node_grad = _combine(ids, received, partner).reshape(node_rows, width)
 
     gathered = [own]
     for shift in range(1, dom_count):

time: 178 us -> 192 us (1.079)
  the two profiles are of different devices: /device:TPU:7 before, /device:TPU:21 now
where the time goes in v3:
time: 192 us; the launch traced here: 190 us
  waiting for transfers between devices  87 us (45%)
  Pallas kernels  33.9 us (18%)
  starting transfers between devices  21.6 us (11%)
  local copies, waits for them, and re-layouts  20.7 us (11%)
  between operations  16.6 us (9%)
  other arithmetic  6.9 us (4%)
  matrix products  3.08 us (2%)
    ppermute x7, waiting for transfers between devices, shards(): gathered.append(lax.ppermute(own, 'dom', pairs))  57.4 us
    ppermute x3, waiting for transfers between devices, shards(): relay.append(lax.ppermute(compact[half + shift], 'dom', within(shift)))  25.6 us
    pallas_call x1, Pallas kernels, _spmm(): pl.pallas_call(_spmm_kernel, out_shape=jax.ShapeDtypeStruct((dests, out_r...  25 us
    unnamed x36, local copies, waits for them, and re-layouts  11.4 us
    ppermute x7, starting transfers between devices, shards(): gathered.append(lax.ppermute(own, 'dom', pairs))  11.1 us
    pallas_call x2, Pallas kernels, _combine(): pl.pallas_call(_combine_kernel, out_shape=jax.ShapeDtypeStruct((out_block...  8.9 us
    slice x1, local copies, waits for them, and re-layouts, shards(): received = [compact[0]]  4.38 us
    ppermute x3, starting transfers between devices, shards(): received.append(lax.ppermute(direct[shift - 1], 'dom', within(shift)))  3.88 us
  transfers between devices with their start and end apart: 21, of which 10 were waited for; matrix products, arithmetic and copies ran while one was open for 10% of the time, Pallas kernels for 16%

profile of v3, /device:TPU:21, one launch (start us, length us, event | category | flops | bytes accessed | tf_op | source)
XLA Modules:
  0.0 189.8 jit_solution(17576408392686525131)
XLA Ops:
  0.7 1.6 convolution_convert_fusion
  2.3 1.3 collective-permute-start
  3.8 1.2 collective-permute-start.2
  23.9 1.4 fusion
  25.3 3.0 %collective-permute-done.1 = bf16[1024,256]{1,0:T(8,128)(2,1)S(1)} collective-permute-done((bf16[1024,256]{1,0:T(8,128)(2,1)S(1)}, bf16[1024,256]{1,0:T(8,128)(2,1)S(1)}, u32[]{:S(2)}, u32[]{:S(2)}) %collective-permute-start.1) | collective-permute-done | bytes 524320 | tf_op jit(solution)/shard_map/ppermute | solution.py:153
  29.0 1.3 collective-permute-start.3
  30.2 25.0 %shard_map.95 = f32[8,584,256]{2,1,0:T(8,128)} custom-call(s32[640]{0:T(1024)S(1)} %get-tuple-element.57.rows_ref, s32[640]{0:T(1024)S(1)} %get-tuple-element.58.slots_ref, s32[1]{0:T(128)} %copy.37.cnt_ref, bf16[640,128,128]{2,1,0:T(8,128)(2,1)} %tv_ref.1, bf16[32,128,256]{2,1,0:T(8,128)(2,1)S(1)} %bitcast.84, f32[8,72,256]{2,1,0:T(8,128)S(1)} %pad.33.extra_ref), custom_call_target="tpu_custom_call" | custom-call | flops 5368709120 | bytes 25755648 | tf_op jit(solution)/shard_map/pallas_call | solution.py:60
  56.6 4.4 %fusion.30 = (f32[1,584,256]{2,1,0:T(8,128)S(1)}, f32[584,256]{1,0:T(8,128)}, f32[584,256]{1,0:T(8,128)}, f32[584,256]{1,0:T(8,128)}, f32[1,584,256]{2,1,0:T(8,1...) fusion(f32[8,584,256]{2,1,0:T(8,128)} %maximum_dynamic-update-slice_fusion), kind=kLoop, calls=%fused_computation.129 | loop fusion | bytes 9568256 | tf_op jit(solution)/shard_map/slice | solution.py:240
  61.5 12.5 %collective-permute-done.6 = f32[584,256]{1,0:T(8,128)S(1)} collective-permute-done((f32[584,256]{1,0:T(8,128)}, f32[584,256]{1,0:T(8,128)S(1)}, u32[]{:S(2)}, u32[]{:S(2)}) %collective-permute-start.6) | collective-permute-done | bytes 598048 | tf_op jit(solution)/shard_map/ppermute | solution.py:230
  73.9 13.2 %collective-permute-done.7 = f32[584,256]{1,0:T(8,128)S(1)} collective-permute-done((f32[584,256]{1,0:T(8,128)}, f32[584,256]{1,0:T(8,128)S(1)}, u32[]{:S(2)}, u32[]{:S(2)}) %collective-permute-start.7) | collective-permute-done | bytes 598048 | tf_op jit(solution)/shard_map/ppermute | solution.py:230
  88.1 1.8 pad_maximum_fusion.recv_ref
  90.9 1.4 constant_dynamic-update-slice_fusion.15
  94.1 4.5 %shard_map.96 = f32[8,128,256]{2,1,0:T(8,128)} custom-call(s32[16]{0:T(128)} %convert_element_type.41.map_ref, f32[4,584,256]{2,1,0:T(8,128)} %copy-done.1, f32[8,128,256]{2,1,0:T(8,128)} %broadcast_in_dim.83.init_ref), custom_call_target="tpu_custom_call" | custom-call | flops 524288 | bytes 4194304 | tf_op jit(solution)/shard_map/pallas_call | solution.py:108
  98.5 3.2 %collective-permute-start.9 = (f32[584,256]{1,0:T(8,128)}, f32[584,256]{1,0:T(8,128)S(1)}, u32[]{:S(2)}, u32[]{:S(2)}) collective-permute-start(f32[584,256]{1,0:T(8,128)} %get-tuple-element.22), channel_id=1, source_target_pairs={{0,4},{4,8},{8,12},{12,0},{16,20},{20,24},{24,28},{28,16},{1,5},{5... | collective-permute-start | bytes 1794056 | tf_op jit(solution)/shard_map/ppermute | solution.py:242
  102.4 1.7 collective-permute-start.12
  104.7 45.7 %collective-permute-done.15 = f32[32,256]{1,0:T(8,128)S(1)} collective-permute-done((f32[32,256]{1,0:T(8,128)}, f32[32,256]{1,0:T(8,128)S(1)}, u32[]{:S(2)}, u32[]{:S(2)}) %collective-permute-start.15) | collective-permute-done | bytes 32800 | tf_op jit(solution)/shard_map/ppermute | solution.py:250
  150.5 4.3 %collective-permute-start.16 = (f32[32,256]{1,0:T(8,128)}, f32[32,256]{1,0:T(8,128)S(1)}, u32[]{:S(2)}, u32[]{:S(2)}) collective-permute-start(f32[32,256]{1,0:T(8,128)} %get-tuple-element.31), channel_id=1, source_target_pairs={{0,12},{4,16},{8,20},{12,24},{16,28},{20,0},{24,4},{28,8},{1,13},{... | collective-permute-start | bytes 98312 | tf_op jit(solution)/shard_map/ppermute | solution.py:250
  156.1 2.9 %collective-permute-start.17 = (f32[32,256]{1,0:T(8,128)}, f32[32,256]{1,0:T(8,128)S(1)}, u32[]{:S(2)}, u32[]{:S(2)}) collective-permute-start(f32[32,256]{1,0:T(8,128)} %get-tuple-element.31), channel_id=1, source_target_pairs={{0,16},{4,20},{8,24},{12,28},{16,0},{20,4},{24,8},{28,12},{1,17},{... | collective-permute-start | bytes 98312 | tf_op jit(solution)/shard_map/ppermute | solution.py:250
  160.5 1.8 collective-permute-start.18
  162.9 3.1 %collective-permute-done.18 = f32[32,256]{1,0:T(8,128)S(1)} collective-permute-done((f32[32,256]{1,0:T(8,128)}, f32[32,256]{1,0:T(8,128)S(1)}, u32[]{:S(2)}, u32[]{:S(2)}) %collective-permute-start.18) | collective-permute-done | bytes 32800 | tf_op jit(solution)/shard_map/ppermute | solution.py:250
  166.8 2.3 %collective-permute-done.19 = f32[32,256]{1,0:T(8,128)S(1)} collective-permute-done((f32[32,256]{1,0:T(8,128)}, f32[32,256]{1,0:T(8,128)S(1)}, u32[]{:S(2)}, u32[]{:S(2)}) %collective-permute-start.19) | collective-permute-done | bytes 32800 | tf_op jit(solution)/shard_map/ppermute | solution.py:250
  169.0 2.0 %collective-permute-start.20 = (f32[32,256]{1,0:T(8,128)}, f32[32,256]{1,0:T(8,128)S(1)}, u32[]{:S(2)}, u32[]{:S(2)}) collective-permute-start(f32[32,256]{1,0:T(8,128)} %get-tuple-element.31), channel_id=1, source_target_pairs={{0,28},{4,0},{8,4},{12,8},{16,12},{20,16},{24,20},{28,24},{1,29},{... | collective-permute-start | bytes 98312 | tf_op jit(solution)/shard_map/ppermute | solution.py:250
  171.6 4.6 %collective-permute-done.20 = f32[32,256]{1,0:T(8,128)S(1)} collective-permute-done((f32[32,256]{1,0:T(8,128)}, f32[32,256]{1,0:T(8,128)S(1)}, u32[]{:S(2)}, u32[]{:S(2)}) %collective-permute-start.20) | collective-permute-done | bytes 32800 | tf_op jit(solution)/shard_map/ppermute | solution.py:250
  185.4 4.4 %shard_map.97 = f32[8,128,256]{2,1,0:T(8,128)} custom-call(s32[16]{0:T(128)} %convert_element_type.43.map_ref, f32[4,584,256]{2,1,0:T(8,128)} %copy-done.2, f32[8,128,256]{2,1,0:T(8,128)} %collective-permute-done.12.init_ref), custom_call_target="tpu_custom_call" | custom-call | flops 524288 | bytes 4194304 | tf_op jit(solution)/shard_map/pallas_call | solution.py:108
  (97 shorter events, 24.7 us)
Async XLA Ops:
  0.6 23.2 %copy-start = (bf16[1024,256]{1,0:T(8,128)(2,1)S(1)}, bf16[1024,256]{1,0:T(8,128)(2,1)}, u32[]{:S(2)}) copy-start(bf16[1024,256]{1,0:T(8,128)(2,1)} %param.12) | copy-start | bytes 1572868
  0.6 23.2 %copy-start.7 = (bf16[1024,256]{1,0:T(8,128)(2,1)S(1)}, bf16[1024,256]{1,0:T(8,128)(2,1)}, u32[]{:S(2)}) copy-start(bf16[1024,256]{1,0:T(8,128)(2,1)} %param.10) | copy-start | bytes 1572868
  2.3 23.0 %collective-permute-start = (bf16[1024,256]{1,0:T(8,128)(2,1)S(1)}, bf16[1024,256]{1,0:T(8,128)(2,1)S(1)}, u32[]{:S(2)}, u32[]{:S(2)}) collective-permute-start(bf16[1024,256]{1,0:T(8,128)(2,1)S(1)} %convolution_convert_fusion), channel_id=1, source_target_pairs={{0,1},{1,2},{2,3},{3,0},{4,5},{5,6},{6,7},{7,4},{8,9},{9,10},{10,1... | collective-permute-start | bytes 1572872 | tf_op jit(solution)/shard_map/ppermute | solution.py:153
  3.6 24.8 %collective-permute-start.1 = (bf16[1024,256]{1,0:T(8,128)(2,1)S(1)}, bf16[1024,256]{1,0:T(8,128)(2,1)S(1)}, u32[]{:S(2)}, u32[]{:S(2)}) collective-permute-start(bf16[1024,256]{1,0:T(8,128)(2,1)S(1)} %convolution_convert_fusion), channel_id=1, source_target_pairs={{0,2},{1,3},{2,0},{3,1},{4,6},{5,7},{6,4},{7,5},{8,10},{9,11},{10,... | collective-permute-start | bytes 1572872 | tf_op jit(solution)/shard_map/ppermute | solution.py:153
  3.8 24.5 %collective-permute-start.2 = (bf16[1024,256]{1,0:T(8,128)(2,1)S(1)}, bf16[1024,256]{1,0:T(8,128)(2,1)S(1)}, u32[]{:S(2)}, u32[]{:S(2)}) collective-permute-start(bf16[1024,256]{1,0:T(8,128)(2,1)S(1)} %convolution_convert_fusion), channel_id=1, source_target_pairs={{0,3},{1,0},{2,1},{3,2},{4,7},{5,4},{6,5},{7,6},{8,11},{9,8},{10,9... | collective-permute-start | bytes 1572872 | tf_op jit(solution)/shard_map/ppermute | solution.py:153
  28.5 26.7 %collective-permute-start.4 = (f32[256,256]{0,1:T(8,128)S(1)}, f32[256,256]{0,1:T(8,128)S(1)}, u32[]{:S(2)}, u32[]{:S(2)}) collective-permute-start(f32[256,256]{0,1:T(8,128)S(1)} %fusion), channel_id=1, source_target_pairs={{0,2},{1,3},{2,0},{3,1},{4,6},{5,7},{6,4},{7,5},{8,10},{9,11},{10,... | collective-permute-start | bytes 786440 | tf_op jit(solution)/shard_map/ppermute | solution.py:161
  28.8 26.5 %collective-permute-start.5 = (f32[256,256]{0,1:T(8,128)S(1)}, f32[256,256]{0,1:T(8,128)S(1)}, u32[]{:S(2)}, u32[]{:S(2)}) collective-permute-start(f32[256,256]{0,1:T(8,128)S(1)} %fusion), channel_id=1, source_target_pairs={{0,3},{1,0},{2,1},{3,2},{4,7},{5,4},{6,5},{7,6},{8,11},{9,8},{10,9... | collective-permute-start | bytes 786440 | tf_op jit(solution)/shard_map/ppermute | solution.py:161
  29.0 26.3 %collective-permute-start.3 = (f32[256,256]{0,1:T(8,128)S(1)}, f32[256,256]{0,1:T(8,128)S(1)}, u32[]{:S(2)}, u32[]{:S(2)}) collective-permute-start(f32[256,256]{0,1:T(8,128)S(1)} %fusion), channel_id=1, source_target_pairs={{0,1},{1,2},{2,3},{3,0},{4,5},{5,6},{6,7},{7,4},{8,9},{9,10},{10,1... | collective-permute-start | bytes 786440 | tf_op jit(solution)/shard_map/ppermute | solution.py:161
  60.9 13.0 %collective-permute-start.6 = (f32[584,256]{1,0:T(8,128)}, f32[584,256]{1,0:T(8,128)S(1)}, u32[]{:S(2)}, u32[]{:S(2)}) collective-permute-start(f32[584,256]{1,0:T(8,128)} %get-tuple-element.43), channel_id=1, source_target_pairs={{0,4},{4,8},{8,12},{12,0},{16,20},{20,24},{24,28},{28,16},{1,5},{5... | collective-permute-start | bytes 1794056 | tf_op jit(solution)/shard_map/ppermute | solution.py:230
  60.9 26.2 %collective-permute-start.7 = (f32[584,256]{1,0:T(8,128)}, f32[584,256]{1,0:T(8,128)S(1)}, u32[]{:S(2)}, u32[]{:S(2)}) collective-permute-start(f32[584,256]{1,0:T(8,128)} %get-tuple-element.42), channel_id=1, source_target_pairs={{0,8},{4,12},{8,0},{12,4},{16,24},{20,28},{24,16},{28,20},{1,9},{5... | collective-permute-start | bytes 1794056 | tf_op jit(solution)/shard_map/ppermute | solution.py:230
  61.0 26.1 %collective-permute-start.8 = (f32[584,256]{1,0:T(8,128)}, f32[584,256]{1,0:T(8,128)S(1)}, u32[]{:S(2)}, u32[]{:S(2)}) collective-permute-start(f32[584,256]{1,0:T(8,128)} %get-tuple-element.41), channel_id=1, source_target_pairs={{0,12},{4,0},{8,4},{12,8},{16,28},{20,16},{24,20},{28,24},{1,13},{... | collective-permute-start | bytes 1794056 | tf_op jit(solution)/shard_map/ppermute | solution.py:230
  73.9 13.3 %copy-start.3 = (f32[584,256]{1,0:T(8,128)}, f32[584,256]{1,0:T(8,128)S(1)}, u32[]{:S(2)}) copy-start(f32[584,256]{1,0:T(8,128)S(1)} %collective-permute-done.6) | copy-start | bytes 1794052
  87.1 3.7 %collective-permute-start.13 = (f32[32,256]{1,0:T(8,128)S(1)}, f32[32,256]{1,0:T(8,128)S(1)}, u32[]{:S(2)}, u32[]{:S(2)}) collective-permute-start(f32[32,256]{1,0:T(8,128)S(1)} %fusion.3), channel_id=1, source_target_pairs={{0,16},{4,20},{8,24},{12,28},{16,0},{20,4},{24,8},{28,12},{1,17},{... | collective-permute-start | bytes 98312 | tf_op jit(solution)/shard_map/ppermute | solution.py:233
  92.3 11.8 %collective-permute-start.14 = (f32[32,256]{1,0:T(8,128)}, f32[32,256]{1,0:T(8,128)S(1)}, u32[]{:S(2)}, u32[]{:S(2)}) collective-permute-start(f32[32,256]{1,0:T(8,128)} %get-tuple-element.31), channel_id=1, source_target_pairs={{0,4},{4,8},{8,12},{12,16},{16,20},{20,24},{24,28},{28,0},{1,5},{5... | collective-permute-start | bytes 98312 | tf_op jit(solution)/shard_map/ppermute | solution.py:250
  98.5 84.5 %collective-permute-start.9 = (f32[584,256]{1,0:T(8,128)}, f32[584,256]{1,0:T(8,128)S(1)}, u32[]{:S(2)}, u32[]{:S(2)}) collective-permute-start(f32[584,256]{1,0:T(8,128)} %get-tuple-element.22), channel_id=1, source_target_pairs={{0,4},{4,8},{8,12},{12,0},{16,20},{20,24},{24,28},{28,16},{1,5},{5... | collective-permute-start | bytes 1794056 | tf_op jit(solution)/shard_map/ppermute | solution.py:242
  101.7 81.3 %collective-permute-start.10 = (f32[584,256]{1,0:T(8,128)}, f32[584,256]{1,0:T(8,128)S(1)}, u32[]{:S(2)}, u32[]{:S(2)}) collective-permute-start(f32[584,256]{1,0:T(8,128)} %get-tuple-element.23), channel_id=1, source_target_pairs={{0,8},{4,12},{8,0},{12,4},{16,24},{20,28},{24,16},{28,20},{1,9},{5... | collective-permute-start | bytes 1794056 | tf_op jit(solution)/shard_map/ppermute | solution.py:242
  102.1 80.8 %collective-permute-start.11 = (f32[584,256]{1,0:T(8,128)}, f32[584,256]{1,0:T(8,128)S(1)}, u32[]{:S(2)}, u32[]{:S(2)}) collective-permute-start(f32[584,256]{1,0:T(8,128)} %get-tuple-element.24), channel_id=1, source_target_pairs={{0,12},{4,0},{8,4},{12,8},{16,28},{20,16},{24,20},{28,24},{1,13},{... | collective-permute-start | bytes 1794056 | tf_op jit(solution)/shard_map/ppermute | solution.py:242
  102.4 82.3 %collective-permute-start.12 = (f32[8,128,256]{2,1,0:T(8,128)}, f32[8,128,256]{2,1,0:T(8,128)}, u32[]{:S(2)}, u32[]{:S(2)}) collective-permute-start(f32[8,128,256]{2,1,0:T(8,128)} %shard_map.96), channel_id=1, source_target_pairs={{0,16},{4,20},{8,24},{12,28},{16,0},{20,4},{24,8},{28,12},{1,17},{... | collective-permute-start | bytes 3145736 | tf_op jit(solution)/shard_map/ppermute | solution.py:239
  104.1 46.3 %collective-permute-start.15 = (f32[32,256]{1,0:T(8,128)}, f32[32,256]{1,0:T(8,128)S(1)}, u32[]{:S(2)}, u32[]{:S(2)}) collective-permute-start(f32[32,256]{1,0:T(8,128)} %get-tuple-element.31), channel_id=1, source_target_pairs={{0,8},{4,12},{8,16},{12,20},{16,24},{20,28},{24,0},{28,4},{1,9},{5... | collective-permute-start | bytes 98312 | tf_op jit(solution)/shard_map/ppermute | solution.py:250
  150.5 5.6 %collective-permute-start.16 = (f32[32,256]{1,0:T(8,128)}, f32[32,256]{1,0:T(8,128)S(1)}, u32[]{:S(2)}, u32[]{:S(2)}) collective-permute-start(f32[32,256]{1,0:T(8,128)} %get-tuple-element.31), channel_id=1, source_target_pairs={{0,12},{4,16},{8,20},{12,24},{16,28},{20,0},{24,4},{28,8},{1,13},{... | collective-permute-start | bytes 98312 | tf_op jit(solution)/shard_map/ppermute | solution.py:250
  156.1 4.4 %collective-permute-start.17 = (f32[32,256]{1,0:T(8,128)}, f32[32,256]{1,0:T(8,128)S(1)}, u32[]{:S(2)}, u32[]{:S(2)}) collective-permute-start(f32[32,256]{1,0:T(8,128)} %get-tuple-element.31), channel_id=1, source_target_pairs={{0,16},{4,20},{8,24},{12,28},{16,0},{20,4},{24,8},{28,12},{1,17},{... | collective-permute-start | bytes 98312 | tf_op jit(solution)/shard_map/ppermute | solution.py:250
  160.5 5.6 %collective-permute-start.18 = (f32[32,256]{1,0:T(8,128)}, f32[32,256]{1,0:T(8,128)S(1)}, u32[]{:S(2)}, u32[]{:S(2)}) collective-permute-start(f32[32,256]{1,0:T(8,128)} %get-tuple-element.31), channel_id=1, source_target_pairs={{0,20},{4,24},{8,28},{12,0},{16,4},{20,8},{24,12},{28,16},{1,21},{... | collective-permute-start | bytes 98312 | tf_op jit(solution)/shard_map/ppermute | solution.py:250
  166.1 3.0 %collective-permute-start.19 = (f32[32,256]{1,0:T(8,128)}, f32[32,256]{1,0:T(8,128)S(1)}, u32[]{:S(2)}, u32[]{:S(2)}) collective-permute-start(f32[32,256]{1,0:T(8,128)} %get-tuple-element.31), channel_id=1, source_target_pairs={{0,24},{4,28},{8,0},{12,4},{16,8},{20,12},{24,16},{28,20},{1,25},{... | collective-permute-start | bytes 98312 | tf_op jit(solution)/shard_map/ppermute | solution.py:250
  169.0 7.2 %collective-permute-start.20 = (f32[32,256]{1,0:T(8,128)}, f32[32,256]{1,0:T(8,128)S(1)}, u32[]{:S(2)}, u32[]{:S(2)}) collective-permute-start(f32[32,256]{1,0:T(8,128)} %get-tuple-element.31), channel_id=1, source_target_pairs={{0,28},{4,0},{8,4},{12,8},{16,12},{20,16},{24,20},{28,24},{1,29},{... | collective-permute-start | bytes 98312 | tf_op jit(solution)/shard_map/ppermute | solution.py:250
  (5 other events, 8.1 us)
